TPU v7x, 256 devices: a whole 4x4x8 slice. The times are simulated.
256 devices in a mesh: ctx: 32 (over y, z_hi, x), uly: 8 (over z_lo, core).
Axes of the slice: x: 4, y: 4, z: 8 (z_hi: 2, z_lo: 4; z = z_hi * 4 + z_lo), core: 2. Of those that a mesh axis runs over, the one named last changes fastest.
Arguments:
- queries: bfloat16 [32768, 4096], P(('ctx', 'uly')), may hold values from -5 to 5
- keys: bfloat16 [32768, 1024], P(('ctx', 'uly')), may hold values from -5 to 5
- values: bfloat16 [32768, 1024], P(('ctx', 'uly')), may hold values from -6 to 6
- output_gradient: bfloat16 [32768, 4096], P(('ctx', 'uly')), may hold values from -6 to 6
- doc_lengths: int32 [32], replicated, may hold values from 1 to 3072, 32768 in all
Outputs:
- grad_queries: bfloat16 [32768, 4096], P(('ctx', 'uly'))
- keys_gradient: bfloat16 [32768, 1024], P(('ctx', 'uly'))
- values_gradient: bfloat16 [32768, 1024], P(('ctx', 'uly'))
Inputs may be any that keep to these rules, and one draw needn't show every extreme that they name: `doc_lengths`: whole documents that fill the sequence; the longest is exactly 3072 tokens.
All inputs are finite; a program needn't handle non-finite values.
Results may differ from a plain program's by a relative error of at most 0.017.
Values may be sent and summed in bfloat16 or wider, within the bound.
No kernel may reach another device: no remote copies, remote signals or barrier semaphores. Data moves between devices by JAX's collectives and lax.ppermute only.
A program may use at most 64 MiB of HBM per device.

v0:
```python
import math

import jax
import jax.numpy as jnp
from jax import lax
from jax.sharding import PartitionSpec as P

HEAD_SIZE = 128
REACH = 3


NEG = -1e30


def from_behind(shard, axis, by):
    length = lax.axis_size(axis)
    pairs = [(i, i + by) for i in range(length) if 0 <= i + by < length]
    return lax.ppermute(shard, axis, pairs)


def fetch_keys(keys, values):
    sources = [(keys, values)]
    for step in range(1, REACH + 1):
        sources.append(from_behind((keys, values), "ctx", step))
    return sources


def tile_mask(q_pos, q_start, k_pos):
    return (k_pos[None, :] <= q_pos[:, None]) & (k_pos[None, :] >= q_start[:, None])


def tile_active(q_pos, q_start, k_pos):
    return (k_pos[0] <= q_pos[-1]) & (k_pos[-1] >= jnp.min(q_start))


def tile_scores(q_tile, k_tile, mask, softmax_scale):
    raw = (
        jnp.einsum("qhgd,khd->hgqk", q_tile, k_tile, preferred_element_type=jnp.float32)
        * softmax_scale
    )
    return jnp.where(mask[None, None], raw, NEG)


def on_device(queries, keys, values, output_gradient, doc_lengths):
    queries, keys, values, output_gradient = (
        lax.all_to_all(queries, "uly", split_axis=1, concat_axis=0, tiled=True),
        lax.all_to_all(keys, "uly", split_axis=1, concat_axis=0, tiled=True),
        lax.all_to_all(values, "uly", split_axis=1, concat_axis=0, tiled=True),
        lax.all_to_all(output_gradient, "uly", split_axis=1, concat_axis=0, tiled=True),
    )
    sources = fetch_keys(keys, values)
    rows = queries.shape[0]
    kv_heads = keys.shape[1] // HEAD_SIZE
    group_members = queries.shape[1] // HEAD_SIZE // kv_heads
    tile = math.gcd(rows, 512)
    count = rows // tile
    softmax_scale = 1.0 / math.sqrt(HEAD_SIZE)
    query_four = queries.reshape(rows, kv_heads, group_members, HEAD_SIZE)
    gradient_four = output_gradient.reshape(rows, kv_heads, group_members, HEAD_SIZE)
    ctx_index = lax.axis_index("ctx")
    local = jnp.arange(rows, dtype=jnp.int32)
    q_pos = ctx_index * rows + local
    ends = jnp.cumsum(doc_lengths)
    q_start = jnp.sum(jnp.where(ends[None, :] <= q_pos[:, None], doc_lengths[None, :], 0), axis=1)
    key_sets = []
    for step, pair in enumerate(sources):
        key_sets.append(
            (
                pair[0].reshape(rows, kv_heads, HEAD_SIZE),
                pair[1].reshape(rows, kv_heads, HEAD_SIZE),
                (ctx_index - step) * rows + local,
            )
        )

    def pieces(index, key_pos):
        q_first = index // count * tile
        k_first = index % count * tile
        q_near = lax.dynamic_slice_in_dim(q_pos, q_first, tile)
        s_near = lax.dynamic_slice_in_dim(q_start, q_first, tile)
        k_near = lax.dynamic_slice_in_dim(key_pos, k_first, tile)
        return (q_first, k_first, q_near, s_near, k_near)

    shape_rows = (kv_heads, group_members, rows)
    forward = (
        jnp.full(shape_rows, NEG, jnp.float32),
        jnp.zeros(shape_rows, jnp.float32),
        jnp.zeros((rows, kv_heads, group_members, HEAD_SIZE), jnp.float32),
    )
    for key_three, value_three, key_pos in key_sets:

        def fwd_step(index, carry, key_three=key_three, value_three=value_three, key_pos=key_pos):
            q_first, k_first, q_near, s_near, k_near = pieces(index, key_pos)

            def fwd_work(state):
                high, total, out_acc = state
                mask = tile_mask(q_near, s_near, k_near)
                scores = tile_scores(
                    lax.dynamic_slice_in_dim(query_four, q_first, tile, 0),
                    lax.dynamic_slice_in_dim(key_three, k_first, tile, 0),
                    mask,
                    softmax_scale,
                )
                old_high = lax.dynamic_slice_in_dim(high, q_first, tile, 2)
                old_total = lax.dynamic_slice_in_dim(total, q_first, tile, 2)
                new_high = jnp.maximum(old_high, jnp.max(scores, axis=3))
                factor = jnp.exp(old_high - new_high)
                terms = jnp.where(mask[None, None], jnp.exp(scores - new_high[..., None]), 0.0)
                new_total = old_total * factor + jnp.sum(terms, axis=3)
                added = jnp.einsum(
                    "hgqk,khd->qhgd",
                    terms.astype(jnp.bfloat16),
                    lax.dynamic_slice_in_dim(value_three, k_first, tile, 0),
                    preferred_element_type=jnp.float32,
                )
                old_out = lax.dynamic_slice_in_dim(out_acc, q_first, tile, 0)
                new_out = old_out * jnp.transpose(factor, (2, 0, 1))[..., None] + added
                return (
                    lax.dynamic_update_slice_in_dim(high, new_high, q_first, 2),
                    lax.dynamic_update_slice_in_dim(total, new_total, q_first, 2),
                    lax.dynamic_update_slice_in_dim(out_acc, new_out, q_first, 0),
                )

            return lax.cond(
                tile_active(q_near, s_near, k_near), fwd_work, lambda state: state, carry
            )

        forward = lax.fori_loop(0, count * count, fwd_step, forward)
    high, total, out_acc = forward
    lse = high + jnp.log(total)
    attn_out = (out_acc / jnp.transpose(total, (2, 0, 1))[..., None]).astype(jnp.bfloat16)
    delta = jnp.transpose(
        jnp.sum(gradient_four.astype(jnp.float32) * attn_out.astype(jnp.float32), axis=3), (1, 2, 0)
    )

    def tile_probs(scores, mask, q_first):
        row_lse = lax.dynamic_slice_in_dim(lse, q_first, tile, 2)
        return jnp.where(mask[None, None], jnp.exp(scores - row_lse[..., None]), 0.0)

    grad_q = jnp.zeros((rows, kv_heads, group_members, HEAD_SIZE), jnp.float32)
    partials = []
    for key_three, value_three, key_pos in key_sets:

        def grad_step(index, carry, key_three=key_three, value_three=value_three, key_pos=key_pos):
            q_first, k_first, q_near, s_near, k_near = pieces(index, key_pos)

            def grad_work(state):
                acc_q, acc_k, acc_v = state
                mask = tile_mask(q_near, s_near, k_near)
                q_tile = lax.dynamic_slice_in_dim(query_four, q_first, tile, 0)
                g_tile = lax.dynamic_slice_in_dim(gradient_four, q_first, tile, 0)
                k_tile = lax.dynamic_slice_in_dim(key_three, k_first, tile, 0)
                v_tile = lax.dynamic_slice_in_dim(value_three, k_first, tile, 0)
                probs = tile_probs(tile_scores(q_tile, k_tile, mask, softmax_scale), mask, q_first)
                probs_b = probs.astype(jnp.bfloat16)
                dprobs = jnp.einsum(
                    "qhgd,khd->hgqk", g_tile, v_tile, preferred_element_type=jnp.float32
                )
                row_delta = lax.dynamic_slice_in_dim(delta, q_first, tile, 2)
                dscores = (probs * (dprobs - row_delta[..., None])).astype(jnp.bfloat16)
                add_q = jnp.einsum(
                    "hgqk,khd->qhgd", dscores, k_tile, preferred_element_type=jnp.float32
                )
                add_k = jnp.einsum(
                    "hgqk,qhgd->khd", dscores, q_tile, preferred_element_type=jnp.float32
                )
                add_v = jnp.einsum(
                    "hgqk,qhgd->khd", probs_b, g_tile, preferred_element_type=jnp.float32
                )
                acc_q = lax.dynamic_update_slice_in_dim(
                    acc_q, lax.dynamic_slice_in_dim(acc_q, q_first, tile, 0) + add_q, q_first, 0
                )
                acc_k = lax.dynamic_update_slice_in_dim(
                    acc_k, lax.dynamic_slice_in_dim(acc_k, k_first, tile, 0) + add_k, k_first, 0
                )
                acc_v = lax.dynamic_update_slice_in_dim(
                    acc_v, lax.dynamic_slice_in_dim(acc_v, k_first, tile, 0) + add_v, k_first, 0
                )
                return (acc_q, acc_k, acc_v)

            return lax.cond(
                tile_active(q_near, s_near, k_near), grad_work, lambda state: state, carry
            )

        empty = jnp.zeros((rows, kv_heads, HEAD_SIZE), jnp.float32)
        grad_q, part_k, part_v = lax.fori_loop(0, count * count, grad_step, (grad_q, empty, empty))
        partials.append((part_k, part_v))
    total_k, total_v = partials[0]
    for step in range(1, REACH + 1):
        returned = (
            from_behind(partials[step][0].astype(jnp.bfloat16), "ctx", -step).astype(jnp.float32),
            from_behind(partials[step][1].astype(jnp.bfloat16), "ctx", -step).astype(jnp.float32),
        )
        total_k = total_k + returned[0]
        total_v = total_v + returned[1]
    out_q = (
        (softmax_scale * grad_q)
        .astype(jnp.bfloat16)
        .reshape(rows, kv_heads * group_members * HEAD_SIZE)
    )
    out_k = (softmax_scale * total_k).astype(jnp.bfloat16).reshape(rows, kv_heads * HEAD_SIZE)
    out_v = total_v.astype(jnp.bfloat16).reshape(rows, kv_heads * HEAD_SIZE)
    return (
        lax.all_to_all(out_q, "uly", split_axis=0, concat_axis=1, tiled=True),
        lax.all_to_all(out_k, "uly", split_axis=0, concat_axis=1, tiled=True),
        lax.all_to_all(out_v, "uly", split_axis=0, concat_axis=1, tiled=True),
    )


def solution(mesh):
    return jax.shard_map(
        on_device,
        mesh=mesh,
        in_specs=(
            P(("ctx", "uly"), None),
            P(("ctx", "uly"), None),
            P(("ctx", "uly"), None),
            P(("ctx", "uly"), None),
            P(),
        ),
        out_specs=(P(("ctx", "uly"), None), P(("ctx", "uly"), None), P(("ctx", "uly"), None)),
        check_vma=False,
    )
```

profile of v0, /device:TPU:22, one launch (start us, length us, event | category | flops | bytes accessed | tf_op | source)
XLA Modules:
  0.0 775.7 jit_solution(1029156044634688322)
XLA Ops:
  2.3 5.9 all-to-all-start
  9.9 8.1 %all-to-all-done = bf16[128,8,128]{2,0,1:T(8,128)(2,1)} async-done(((bf16[128,8,128]{2,0,1:T(8,128)(2,1)}), bf16[128,8,128]{2,0,1:T(8,128)(2,1)}, u32[]{:S(2)}, u32[]{:S(2)}) %all-to-all-start) | async-done | bytes 262176 | tf_op jit(solution)/shard_map/all_to_all | solution.py:47
  18.1 3.4 all-to-all-start.2
  23.8 7.4 all-to-all-done.2
  31.2 3.6 all-to-all-start.1
  34.8 7.4 collective-permute-start.5
  42.2 3.9 collective-permute-start.3
  46.1 4.0 collective-permute-start.1
  51.8 6.5 collective-permute-start.4
  58.3 4.3 collective-permute-start.2
  63.5 33.2 %collective-permute-done.5 = bf16[1024,128]{1,0:T(8,128)(2,1)S(1)} collective-permute-done((bf16[1024,128]{1,0:T(8,128)(2,1)S(1)}, bf16[1024,128]{1,0:T(8,128)(2,1)S(1)}, u32[]{:S(2)}, u32[]{:S(2)}) %collective-permute-start.5) | collective-permute-done | bytes 262176 | tf_op jit(solution)/shard_map/ppermute | solution.py:18
  99.5 2.8 collective-permute-done.3
  104.1 3.9 collective-permute-done.1
  109.8 20.3 %all-to-all-done.1 = bf16[128,8,512]{0,2,1:T(8,128)(2,1)S(1)} async-done(((bf16[128,8,512]{0,2,1:T(8,128)(2,1)}), bf16[128,8,512]{0,2,1:T(8,128)(2,1)S(1)}, u32[]{:S(2)}, u32[]{:S(2)}) %all-to-all-start.1) | async-done | bytes 1048608 | tf_op jit(solution)/shard_map/all_to_all | solution.py:46
  130.0 4.8 all-to-all-start.3
  140.1 50.0 %while.152 = (s32[]{:T(128)}, f32[1,4,1024]{2,1,0:T(4,128)S(1)}, f32[1,4,1024]{2,1,0:T(4,128)S(1)}, f32[1024,1,4,128]{0,3,2,1:T(8,128)}, s32[1024]{0:T(1024)S(1)...) while((s32[]{:T(128)}, f32[1,4,1024]{2,1,0:T(4,128)S(1)}, ...), condition=%wide.region_8.9_spmd, body=%wide.region_2.8_spmd.sunk | while | flops 551819776 | bytes 28216016 | solution.py:127
  144.5 11.4 %conditional.16 = ((f32[1,4,1024]{2,1,0:T(4,128)S(1)}, f32[1,4,1024]{2,1,0:T(4,128)S(1)}, f32[1024,1,4,128]{0,3,2,1:T(8,128)})) conditional(s32[]{:T(128)} %convert_element_type.284, (f32[1,4,1024]{2,1,0:T(4,128)S(1)}, f32[1,4,1024]{2,1,0:T(4,128)S(1)}, f32[1024,1,4,128]{0,3,2,1:T(8,128)}) %tuple.415, (s32[]{:T(128)}, f32[1,4,1024]{2,1,0:T(4,128)S(1)}, ...), branch_computations={%region_4.4_spmd, %region_5.7_spmd} | conditional | flops 551819264 | bytes 28203200 | solution.py:123
  150.1 5.7 dynamic_update_slice.50
  164.7 10.5 %conditional.16 = ((f32[1,4,1024]{2,1,0:T(4,128)S(1)}, f32[1,4,1024]{2,1,0:T(4,128)S(1)}, f32[1024,1,4,128]{0,3,2,1:T(8,128)})) conditional(s32[]{:T(128)} %convert_element_type.284, (f32[1,4,1024]{2,1,0:T(4,128)S(1)}, f32[1,4,1024]{2,1,0:T(4,128)S(1)}, f32[1024,1,4,128]{0,3,2,1:T(8,128)}) %tuple.415, (s32[]{:T(128)}, f32[1,4,1024]{2,1,0:T(4,128)S(1)}, ...), branch_computations={%region_4.4_spmd, %region_5.7_spmd} | conditional | flops 551819264 | bytes 28203200 | solution.py:123
  170.2 5.0 dynamic_update_slice.50
  179.6 10.5 %conditional.16 = ((f32[1,4,1024]{2,1,0:T(4,128)S(1)}, f32[1,4,1024]{2,1,0:T(4,128)S(1)}, f32[1024,1,4,128]{0,3,2,1:T(8,128)})) conditional(s32[]{:T(128)} %convert_element_type.284, (f32[1,4,1024]{2,1,0:T(4,128)S(1)}, f32[1,4,1024]{2,1,0:T(4,128)S(1)}, f32[1024,1,4,128]{0,3,2,1:T(8,128)}) %tuple.415, (s32[]{:T(128)}, f32[1,4,1024]{2,1,0:T(4,128)S(1)}, ...), branch_computations={%region_4.4_spmd, %region_5.7_spmd} | conditional | flops 551819264 | bytes 28203200 | solution.py:123
  185.1 5.0 dynamic_update_slice.50
  190.1 38.5 %while.153 = (s32[]{:T(128)}, f32[1,4,1024]{2,1,0:T(4,128)S(1)}, f32[1,4,1024]{2,1,0:T(4,128)S(1)}, f32[1024,1,4,128]{0,3,2,1:T(8,128)}, s32[1024]{0:T(1024)S(1)...) while((s32[]{:T(128)}, f32[1,4,1024]{2,1,0:T(4,128)S(1)}, ...), condition=%wide.region_15.16_spmd, body=%wide.region_9.15_spmd.sunk | while | flops 551819776 | bytes 28216028 | solution.py:127
  194.5 10.3 %conditional.17 = ((f32[1,4,1024]{2,1,0:T(4,128)S(1)}, f32[1,4,1024]{2,1,0:T(4,128)S(1)}, f32[1024,1,4,128]{0,3,2,1:T(8,128)})) conditional(s32[]{:T(128)} %convert_element_type.285, (f32[1,4,1024]{2,1,0:T(4,128)S(1)}, f32[1,4,1024]{2,1,0:T(4,128)S(1)}, f32[1024,1,4,128]{0,3,2,1:T(8,128)}) %tuple.420, (s32[]{:T(128)}, ...), branch_computations={%region_11.11_spmd, %region_12.14_spmd} | conditional | flops 551819264 | bytes 28203200 | solution.py:123
  199.1 5.7 dynamic_update_slice.53
  209.3 10.3 %conditional.17 = ((f32[1,4,1024]{2,1,0:T(4,128)S(1)}, f32[1,4,1024]{2,1,0:T(4,128)S(1)}, f32[1024,1,4,128]{0,3,2,1:T(8,128)})) conditional(s32[]{:T(128)} %convert_element_type.285, (f32[1,4,1024]{2,1,0:T(4,128)S(1)}, f32[1,4,1024]{2,1,0:T(4,128)S(1)}, f32[1024,1,4,128]{0,3,2,1:T(8,128)}) %tuple.420, (s32[]{:T(128)}, ...), branch_computations={%region_11.11_spmd, %region_12.14_spmd} | conditional | flops 551819264 | bytes 28203200 | solution.py:123
  213.9 5.7 dynamic_update_slice.53
  229.3 29.6 %while.154 = (s32[]{:T(128)}, f32[1,4,1024]{2,1,0:T(4,128)S(1)}, f32[1,4,1024]{2,1,0:T(4,128)S(1)}, f32[1024,1,4,128]{0,3,2,1:T(8,128)}, s32[1024]{0:T(1024)S(1)...) while((s32[]{:T(128)}, f32[1,4,1024]{2,1,0:T(4,128)S(1)}, ...), condition=%wide.region_22.23_spmd, body=%wide.region_16.22_spmd.sunk | while | flops 551819776 | bytes 28216028 | solution.py:127
  239.0 10.3 %conditional.18 = ((f32[1,4,1024]{2,1,0:T(4,128)S(1)}, f32[1,4,1024]{2,1,0:T(4,128)S(1)}, f32[1024,1,4,128]{0,3,2,1:T(8,128)})) conditional(s32[]{:T(128)} %convert_element_type.286, (f32[1,4,1024]{2,1,0:T(4,128)S(1)}, f32[1,4,1024]{2,1,0:T(4,128)S(1)}, f32[1024,1,4,128]{0,3,2,1:T(8,128)}) %tuple.425, (s32[]{:T(128)}, ...), branch_computations={%region_18.18_spmd, %region_19.21_spmd} | conditional | flops 551819264 | bytes 28203200 | solution.py:123
  243.6 5.7 dynamic_update_slice.56
  258.9 3.0 copy.255
  264.8 18.7 %while.155 = (s32[]{:T(128)}, f32[1,4,1024]{2,1,0:T(4,128)S(1)}, f32[1,4,1024]{2,1,0:T(4,128)S(1)}, f32[1024,1,4,128]{0,3,2,1:T(8,128)}, s32[1024]{0:T(1024)S(1)...) while((s32[]{:T(128)}, f32[1,4,1024]{2,1,0:T(4,128)S(1)}, ...), condition=%wide.region_29.30_spmd, body=%wide.region_23.29_spmd.sunk | while | flops 551819776 | bytes 27167424 | solution.py:127
  288.3 71.3 %while.156 = (s32[]{:T(128)}, f32[1024,1,4,128]{0,3,2,1:T(8,128)S(1)}, f32[1024,1,128]{0,2,1:T(8,128)}, f32[1024,1,128]{0,2,1:T(8,128)}, s32[1024]{0:T(1024)S(1)...) while((s32[]{:T(128)}, ...), condition=%wide.region_35.36_spmd, body=%wide.region_31.35_spmd.sunk | while | flops 1355940352 | bytes 37956428 | solution.py:185
  293.0 17.7 %conditional.20 = ((f32[1024,1,4,128]{0,3,2,1:T(8,128)S(1)}, f32[1024,1,128]{0,2,1:T(8,128)}, f32[1024,1,128]{0,2,1:T(8,128)})) conditional(s32[]{:T(128)} %convert_element_type.288, (f32[1024,1,4,128]{0,3,2,1:T(8,128)S(1)}, f32[1024,1,128]{0,2,1:T(8,128)}, f32[1024,1,128]{0,2,1:T(8,128)}) %tuple.435, (s32[]{:T(128)}, ...), branch_computations={%region_33.33_spmd, %region_34.34_spmd} | conditional | flops 1355939840 | bytes 37943564 | solution.py:180
  300.2 2.5 fusion.121
  306.3 4.4 dynamic_update_slice.60
  319.8 17.7 %conditional.20 = ((f32[1024,1,4,128]{0,3,2,1:T(8,128)S(1)}, f32[1024,1,128]{0,2,1:T(8,128)}, f32[1024,1,128]{0,2,1:T(8,128)})) conditional(s32[]{:T(128)} %convert_element_type.288, (f32[1024,1,4,128]{0,3,2,1:T(8,128)S(1)}, f32[1024,1,128]{0,2,1:T(8,128)}, f32[1024,1,128]{0,2,1:T(8,128)}) %tuple.435, (s32[]{:T(128)}, ...), branch_computations={%region_33.33_spmd, %region_34.34_spmd} | conditional | flops 1355939840 | bytes 37943564 | solution.py:180
  327.0 2.5 fusion.121
  333.1 4.4 dynamic_update_slice.60
  342.0 17.5 %conditional.20 = ((f32[1024,1,4,128]{0,3,2,1:T(8,128)S(1)}, f32[1024,1,128]{0,2,1:T(8,128)}, f32[1024,1,128]{0,2,1:T(8,128)})) conditional(s32[]{:T(128)} %convert_element_type.288, (f32[1024,1,4,128]{0,3,2,1:T(8,128)S(1)}, f32[1024,1,128]{0,2,1:T(8,128)}, f32[1024,1,128]{0,2,1:T(8,128)}) %tuple.435, (s32[]{:T(128)}, ...), branch_computations={%region_33.33_spmd, %region_34.34_spmd} | conditional | flops 1355939840 | bytes 37943564 | solution.py:180
  349.2 2.5 fusion.121
  355.1 4.4 dynamic_update_slice.60
  361.3 54.5 %while.157 = (s32[]{:T(128)}, f32[1024,1,4,128]{0,3,2,1:T(8,128)S(1)}, f32[1024,1,128]{0,2,1:T(8,128)}, f32[1024,1,128]{0,2,1:T(8,128)}, s32[1024]{0:T(1024)S(1)...) while((s32[]{:T(128)}, ...), condition=%wide.region_40.41_spmd, body=%wide.region_36.40_spmd.sunk | while | flops 1355940352 | bytes 37956440 | solution.py:185
  366.2 17.8 %conditional.21 = ((f32[1024,1,4,128]{0,3,2,1:T(8,128)S(1)}, f32[1024,1,128]{0,2,1:T(8,128)}, f32[1024,1,128]{0,2,1:T(8,128)})) conditional(s32[]{:T(128)} %convert_element_type.289, (f32[1024,1,4,128]{0,3,2,1:T(8,128)S(1)}, f32[1024,1,128]{0,2,1:T(8,128)}, f32[1024,1,128]{0,2,1:T(8,128)}) %tuple.440, (s32[]{:T(128)}, ...), branch_computations={%region_38.38_spmd, %region_39.39_spmd} | conditional | flops 1355939840 | bytes 37943564 | solution.py:180
  370.7 2.8 fusion.160
  379.6 4.4 dynamic_update_slice.63
  388.7 17.6 %conditional.21 = ((f32[1024,1,4,128]{0,3,2,1:T(8,128)S(1)}, f32[1024,1,128]{0,2,1:T(8,128)}, f32[1024,1,128]{0,2,1:T(8,128)})) conditional(s32[]{:T(128)} %convert_element_type.289, (f32[1024,1,4,128]{0,3,2,1:T(8,128)S(1)}, f32[1024,1,128]{0,2,1:T(8,128)}, f32[1024,1,128]{0,2,1:T(8,128)}) %tuple.440, (s32[]{:T(128)}, ...), branch_computations={%region_38.38_spmd, %region_39.39_spmd} | conditional | flops 1355939840 | bytes 37943564 | solution.py:180
  393.2 2.8 fusion.160
  401.9 4.4 dynamic_update_slice.63
  417.5 36.7 %while.158 = (s32[]{:T(128)}, f32[1024,1,4,128]{0,3,2,1:T(8,128)S(1)}, f32[1024,1,128]{0,2,1:T(8,128)}, f32[1024,1,128]{0,2,1:T(8,128)}, s32[1024]{0:T(1024)S(1)...) while((s32[]{:T(128)}, ...), condition=%wide.region_45.46_spmd, body=%wide.region_41.45_spmd.sunk | while | flops 1355940352 | bytes 37956440 | solution.py:185
  427.3 17.6 %conditional.22 = ((f32[1024,1,4,128]{0,3,2,1:T(8,128)S(1)}, f32[1024,1,128]{0,2,1:T(8,128)}, f32[1024,1,128]{0,2,1:T(8,128)})) conditional(s32[]{:T(128)} %convert_element_type.290, (f32[1024,1,4,128]{0,3,2,1:T(8,128)S(1)}, f32[1024,1,128]{0,2,1:T(8,128)}, f32[1024,1,128]{0,2,1:T(8,128)}) %tuple.445, (s32[]{:T(128)}, ...), branch_computations={%region_43.43_spmd, %region_44.44_spmd} | conditional | flops 1355939840 | bytes 37943564 | solution.py:180
  431.8 2.8 fusion.215
  440.5 4.4 dynamic_update_slice.66
  459.6 19.6 %while.159 = (s32[]{:T(128)}, f32[1024,1,4,128]{0,3,2,1:T(8,128)S(1)}, f32[1024,1,128]{0,2,1:T(8,128)}, f32[1024,1,128]{0,2,1:T(8,128)}, s32[1024]{0:T(1024)S(1)...) while((s32[]{:T(128)}, ...), condition=%wide.region_50.51_spmd, body=%wide.region_46.50_spmd.sunk | while | flops 1355940352 | bytes 39005044 | solution.py:185
  484.8 174.2 %collective-permute-start.7 = (bf16[1024,1,128]{0,2,1:T(8,128)(2,1)S(1)}, bf16[1024,1,128]{0,2,1:T(8,128)(2,1)S(1)}, u32[]{:S(2)}, u32[]{:S(2)}) collective-permute-start(bf16[1024,1,128]{0,2,1:T(8,128)(2,1)S(1)} %convert_element_type.182), channel_id=1, source_target_pairs={{16,0},{24,8},{32,16},{40,24},{48,32},{56,40},{64,48},{72,56},{80,... | collective-permute-start | bytes 786440 | tf_op jit(solution)/shard_map/ppermute | solution.py:18
  666.7 8.2 %collective-permute-done.8 = bf16[1024,1,128]{0,2,1:T(8,128)(2,1)S(1)} collective-permute-done((bf16[1024,1,128]{0,2,1:T(8,128)(2,1)S(1)}, bf16[1024,1,128]{0,2,1:T(8,128)(2,1)S(1)}, u32[]{:S(2)}, u32[]{:S(2)}) %collective-permute-start.8) | collective-permute-done | bytes 262176 | tf_op jit(solution)/shard_map/ppermute | solution.py:18
  674.9 4.9 collective-permute-done.11
  679.8 10.1 %collective-permute-done.9 = bf16[1024,1,128]{0,2,1:T(8,128)(2,1)S(1)} collective-permute-done((bf16[1024,1,128]{0,2,1:T(8,128)(2,1)S(1)}, bf16[1024,1,128]{0,2,1:T(8,128)(2,1)S(1)}, u32[]{:S(2)}, u32[]{:S(2)}) %collective-permute-start.9) | collective-permute-done | bytes 262176 | tf_op jit(solution)/shard_map/ppermute | solution.py:18
  693.7 26.3 %all-to-all-start.6 = ((bf16[8,128,128]{2,1,0:T(8,128)(2,1)}), bf16[8,128,128]{2,1,0:T(8,128)(2,1)S(1)}, u32[]{:S(2)}, u32[]{:S(2)}) async-start(bf16[8,128,128]{2,1,0:T(8,128)(2,1)} %bitcast.197), calls=%async_computation.6 | async-start | bytes 524288 | tf_op jit(solution)/shard_map/all_to_all | solution.py:205
  720.8 8.9 %all-to-all-done.6 = bf16[8,128,128]{2,1,0:T(8,128)(2,1)S(1)} async-done(((bf16[8,128,128]{2,1,0:T(8,128)(2,1)}), bf16[8,128,128]{2,1,0:T(8,128)(2,1)S(1)}, u32[]{:S(2)}, u32[]{:S(2)}) %all-to-all-start.6) | async-done | bytes 262176 | tf_op jit(solution)/shard_map/all_to_all | solution.py:205
  729.7 4.0 all-to-all-start.5
  735.8 7.7 all-to-all-done.5
  743.5 3.6 all-to-all-start.4
  750.1 23.5 %all-to-all-done.4 = bf16[8,128,512]{2,1,0:T(8,128)(2,1)S(1)} async-done(((bf16[8,128,512]{2,1,0:T(8,128)(2,1)}), bf16[8,128,512]{2,1,0:T(8,128)(2,1)S(1)}, u32[]{:S(2)}, u32[]{:S(2)}) %all-to-all-start.4) | async-done | bytes 1048608 | tf_op jit(solution)/shard_map/all_to_all | solution.py:203
  (432 shorter events, 220.8 us)
Async XLA Ops:
  0.6 49.5 %copy-start.40 = (s32[32]{0:T(128)S(1)}, s32[32]{0:T(128)}, u32[]{:S(2)}) copy-start(s32[32]{0:T(128)} %param.41) | copy-start | bytes 388
  1.6 48.8 %copy-start.23 = (bf16[128,4096]{1,0:T(8,128)(2,1)S(1)}, bf16[128,4096]{1,0:T(8,128)(2,1)}, u32[]{:S(2)}) copy-start(bf16[128,4096]{1,0:T(8,128)(2,1)} %param.40) | copy-start | bytes 3145732
  2.3 15.8 %all-to-all-start = ((bf16[128,8,128]{2,0,1:T(8,128)(2,1)}), bf16[128,8,128]{2,0,1:T(8,128)(2,1)}, u32[]{:S(2)}, u32[]{:S(2)}) async-start(bf16[128,8,128]{2,0,1:T(8,128)(2,1)} %copy_bitcast_fusion.1), calls=%async_computation | async-start | bytes 524288 | tf_op jit(solution)/shard_map/all_to_all | solution.py:47
  18.1 13.1 %all-to-all-start.2 = ((bf16[128,8,128]{2,0,1:T(8,128)(2,1)}), bf16[128,8,128]{2,0,1:T(8,128)(2,1)S(1)}, u32[]{:S(2)}, u32[]{:S(2)}) async-start(bf16[128,8,128]{2,0,1:T(8,128)(2,1)} %copy_bitcast_fusion), calls=%async_computation.2 | async-start | bytes 524288 | tf_op jit(solution)/shard_map/all_to_all | solution.py:48
  31.2 98.9 %copy-start.28 = (bf16[128,8,128]{2,0,1:T(8,128)(2,1)}, bf16[128,8,128]{2,0,1:T(8,128)(2,1)S(1)}, u32[]{:S(2)}) copy-start(bf16[128,8,128]{2,0,1:T(8,128)(2,1)S(1)} %all-to-all-done.2) | copy-start | bytes 786436
  31.2 98.9 %all-to-all-start.1 = ((bf16[128,8,512]{0,2,1:T(8,128)(2,1)}), bf16[128,8,512]{0,2,1:T(8,128)(2,1)S(1)}, u32[]{:S(2)}, u32[]{:S(2)}) async-start(bf16[128,8,512]{0,2,1:T(8,128)(2,1)} %bitcast.171), calls=%async_computation.1 | async-start | bytes 2097152 | tf_op jit(solution)/shard_map/all_to_all | solution.py:46
  34.8 61.9 %collective-permute-start.5 = (bf16[1024,128]{1,0:T(8,128)(2,1)S(1)}, bf16[1024,128]{1,0:T(8,128)(2,1)S(1)}, u32[]{:S(2)}, u32[]{:S(2)}) collective-permute-start(bf16[1024,128]{1,0:T(8,128)(2,1)S(1)} %bitcast.731), channel_id=1, source_target_pairs={{0,24},{8,32},{16,40},{24,48},{32,56},{40,64},{48,72},{56,80},{64,... | collective-permute-start | bytes 786440 | tf_op jit(solution)/shard_map/ppermute | solution.py:18
  42.2 60.1 %collective-permute-start.3 = (bf16[1024,128]{1,0:T(8,128)(2,1)S(1)}, bf16[1024,128]{1,0:T(8,128)(2,1)}, u32[]{:S(2)}, u32[]{:S(2)}) collective-permute-start(bf16[1024,128]{1,0:T(8,128)(2,1)S(1)} %bitcast.732), channel_id=1, source_target_pairs={{0,16},{8,24},{16,32},{24,40},{32,48},{40,56},{48,64},{56,72},{64,... | collective-permute-start | bytes 786440 | tf_op jit(solution)/shard_map/ppermute | solution.py:18
  46.1 61.9 %collective-permute-start.1 = (bf16[1024,128]{1,0:T(8,128)(2,1)S(1)}, bf16[1024,128]{1,0:T(8,128)(2,1)}, u32[]{:S(2)}, u32[]{:S(2)}) collective-permute-start(bf16[1024,128]{1,0:T(8,128)(2,1)S(1)} %bitcast.733), channel_id=1, source_target_pairs={{0,8},{8,16},{16,24},{24,32},{32,40},{40,48},{48,56},{56,64},{64,7... | collective-permute-start | bytes 786440 | tf_op jit(solution)/shard_map/ppermute | solution.py:18
  51.8 212.9 %collective-permute-start.4 = (bf16[1024,128]{1,0:T(8,128)(2,1)}, bf16[1024,128]{1,0:T(8,128)(2,1)S(1)}, u32[]{:S(2)}, u32[]{:S(2)}) collective-permute-start(bf16[1024,128]{1,0:T(8,128)(2,1)} %bitcast.176), channel_id=1, source_target_pairs={{0,24},{8,32},{16,40},{24,48},{32,56},{40,64},{48,72},{56,80},{64,... | collective-permute-start | bytes 786440 | tf_op jit(solution)/shard_map/ppermute | solution.py:18
  58.3 170.3 %collective-permute-start.2 = (bf16[1024,128]{1,0:T(8,128)(2,1)}, bf16[1024,128]{1,0:T(8,128)(2,1)S(1)}, u32[]{:S(2)}, u32[]{:S(2)}) collective-permute-start(bf16[1024,128]{1,0:T(8,128)(2,1)} %bitcast.176), channel_id=1, source_target_pairs={{0,16},{8,24},{16,32},{24,40},{32,48},{40,56},{48,64},{56,72},{64,... | collective-permute-start | bytes 786440 | tf_op jit(solution)/shard_map/ppermute | solution.py:18
  96.7 41.8 %copy-start.32 = (bf16[1024,128]{1,0:T(8,128)(2,1)}, bf16[1024,128]{1,0:T(8,128)(2,1)S(1)}, u32[]{:S(2)}) copy-start(bf16[1024,128]{1,0:T(8,128)(2,1)S(1)} %collective-permute-done.5) | copy-start | bytes 786436
  96.7 93.4 %collective-permute-start = (bf16[1024,128]{1,0:T(8,128)(2,1)}, bf16[1024,128]{1,0:T(8,128)(2,1)S(1)}, u32[]{:S(2)}, u32[]{:S(2)}) collective-permute-start(bf16[1024,128]{1,0:T(8,128)(2,1)} %bitcast.176), channel_id=1, source_target_pairs={{0,8},{8,16},{16,24},{24,32},{32,40},{40,48},{48,56},{56,64},{64,7... | collective-permute-start | bytes 786440 | tf_op jit(solution)/shard_map/ppermute | solution.py:18
  130.0 128.9 %all-to-all-start.3 = ((bf16[128,8,512]{0,2,1:T(8,128)(2,1)}), bf16[128,8,512]{0,2,1:T(8,128)(2,1)}, u32[]{:S(2)}, u32[]{:S(2)}) async-start(bf16[128,8,512]{0,2,1:T(8,128)(2,1)} %bitcast.186), calls=%async_computation.3 | async-start | bytes 2097152 | tf_op jit(solution)/shard_map/all_to_all | solution.py:49
  144.8 3.2 copy-start.14
  144.8 3.2 copy-start.37
  165.0 3.2 copy-start.14
  165.0 3.2 copy-start.37
  179.9 3.2 copy-start.14
  179.9 3.2 copy-start.37
  194.8 2.1 copy-start.15
  194.9 2.1 copy-start.36
  209.6 2.1 copy-start.15
  209.6 2.1 copy-start.36
  239.3 2.1 copy-start.16
  239.3 2.1 copy-start.35
  258.9 5.9 copy-start.4
  258.9 5.9 copy-start.34
  283.5 3.7 copy-start.2
  293.0 2.1 copy-start.21
  293.0 2.1 copy-start.24
  295.1 2.4 copy-start.29
  319.8 2.1 copy-start.21
  319.8 2.1 copy-start.24
  321.9 2.4 copy-start.29
  342.0 2.1 copy-start.21
  342.0 2.1 copy-start.24
  344.1 2.4 copy-start.29
  366.2 2.1 copy-start.19
  366.2 2.1 copy-start.25
  370.7 2.8 copy-start.9
  370.7 3.7 copy-start.7
  388.7 2.1 copy-start.19
  393.2 2.8 copy-start.9
  393.2 3.7 copy-start.7
  417.5 42.1 %copy-start.39 = (s32[1024]{0:T(1024)S(1)}, s32[1024]{0:T(1024)}, u32[]{:S(2)}) copy-start(s32[1024]{0:T(1024)} %copy-done.38) | copy-start | bytes 12292
  427.3 2.1 copy-start.20
  427.3 2.1 copy-start.26
  431.8 2.8 copy-start.10
  431.8 3.7 copy-start.5
  456.0 208.8 %collective-permute-start.6 = (bf16[1024,1,128]{0,2,1:T(8,128)(2,1)}, bf16[1024,1,128]{0,2,1:T(8,128)(2,1)}, u32[]{:S(2)}, u32[]{:S(2)}) collective-permute-start(bf16[1024,1,128]{0,2,1:T(8,128)(2,1)} %convert_element_type.180), channel_id=1, source_target_pairs={{8,0},{16,8},{24,16},{32,24},{40,32},{48,40},{56,48},{64,56},{72,6... | collective-permute-start | bytes 786440 | tf_op jit(solution)/shard_map/ppermute | solution.py:18
  479.3 210.6 %copy-start.12 = (f32[1024,1,128]{0,2,1:T(8,128)S(1)}, f32[1024,1,128]{0,2,1:T(8,128)}, u32[]{:S(2)}) copy-start(f32[1024,1,128]{0,2,1:T(8,128)} %get-tuple-element.2763) | copy-start | bytes 1572868
  479.3 210.6 %copy-start.22 = (f32[1024,1,128]{0,2,1:T(8,128)S(1)}, f32[1024,1,128]{0,2,1:T(8,128)}, u32[]{:S(2)}) copy-start(f32[1024,1,128]{0,2,1:T(8,128)} %get-tuple-element.2767) | copy-start | bytes 1572868
  484.8 181.9 %collective-permute-start.7 = (bf16[1024,1,128]{0,2,1:T(8,128)(2,1)S(1)}, bf16[1024,1,128]{0,2,1:T(8,128)(2,1)S(1)}, u32[]{:S(2)}, u32[]{:S(2)}) collective-permute-start(bf16[1024,1,128]{0,2,1:T(8,128)(2,1)S(1)} %convert_element_type.182), channel_id=1, source_target_pairs={{16,0},{24,8},{32,16},{40,24},{48,32},{56,40},{64,48},{72,56},{80,... | collective-permute-start | bytes 786440 | tf_op jit(solution)/shard_map/ppermute | solution.py:18
  659.0 15.9 %collective-permute-start.8 = (bf16[1024,1,128]{0,2,1:T(8,128)(2,1)S(1)}, bf16[1024,1,128]{0,2,1:T(8,128)(2,1)S(1)}, u32[]{:S(2)}, u32[]{:S(2)}) collective-permute-start(bf16[1024,1,128]{0,2,1:T(8,128)(2,1)S(1)} %convert_element_type.184), channel_id=1, source_target_pairs={{24,0},{32,8},{40,16},{48,24},{56,32},{64,40},{72,48},{80,56},{88,... | collective-permute-start | bytes 786440 | tf_op jit(solution)/shard_map/ppermute | solution.py:18
  660.9 18.9 %collective-permute-start.11 = (bf16[1024,1,128]{0,2,1:T(8,128)(2,1)S(1)}, bf16[1024,1,128]{0,2,1:T(8,128)(2,1)S(1)}, u32[]{:S(2)}, u32[]{:S(2)}) collective-permute-start(bf16[1024,1,128]{0,2,1:T(8,128)(2,1)S(1)} %convert_element_type.191), channel_id=1, source_target_pairs={{24,0},{32,8},{40,16},{48,24},{56,32},{64,40},{72,48},{80,56},{88,... | collective-permute-start | bytes 786440 | tf_op jit(solution)/shard_map/ppermute | solution.py:18
  662.8 17.0 %collective-permute-start.10 = (bf16[1024,1,128]{0,2,1:T(8,128)(2,1)S(1)}, bf16[1024,1,128]{0,2,1:T(8,128)(2,1)S(1)}, u32[]{:S(2)}, u32[]{:S(2)}) collective-permute-start(bf16[1024,1,128]{0,2,1:T(8,128)(2,1)S(1)} %convert_element_type.189), channel_id=1, source_target_pairs={{16,0},{24,8},{32,16},{40,24},{48,32},{56,40},{64,48},{72,56},{80,... | collective-permute-start | bytes 786440 | tf_op jit(solution)/shard_map/ppermute | solution.py:18
  664.8 25.1 %collective-permute-start.9 = (bf16[1024,1,128]{0,2,1:T(8,128)(2,1)S(1)}, bf16[1024,1,128]{0,2,1:T(8,128)(2,1)S(1)}, u32[]{:S(2)}, u32[]{:S(2)}) collective-permute-start(bf16[1024,1,128]{0,2,1:T(8,128)(2,1)S(1)} %convert_element_type.187), channel_id=1, source_target_pairs={{8,0},{16,8},{24,16},{32,24},{40,32},{48,40},{56,48},{64,56},{72,6... | collective-permute-start | bytes 786440 | tf_op jit(solution)/shard_map/ppermute | solution.py:18
  693.7 36.0 %all-to-all-start.6 = ((bf16[8,128,128]{2,1,0:T(8,128)(2,1)}), bf16[8,128,128]{2,1,0:T(8,128)(2,1)S(1)}, u32[]{:S(2)}, u32[]{:S(2)}) async-start(bf16[8,128,128]{2,1,0:T(8,128)(2,1)} %bitcast.197), calls=%async_computation.6 | async-start | bytes 524288 | tf_op jit(solution)/shard_map/all_to_all | solution.py:205
  729.7 4.1 copy-start.30
  729.7 13.8 %all-to-all-start.5 = ((bf16[8,128,128]{2,1,0:T(8,128)(2,1)}), bf16[8,128,128]{2,1,0:T(8,128)(2,1)}, u32[]{:S(2)}, u32[]{:S(2)}) async-start(bf16[8,128,128]{2,1,0:T(8,128)(2,1)} %bitcast.194), calls=%async_computation.5 | async-start | bytes 524288 | tf_op jit(solution)/shard_map/all_to_all | solution.py:204
  733.8 13.3 %copy-start.31 = (bf16[8,128,128]{2,1,0:T(8,128)(2,1)S(1)}, bf16[8,128,128]{2,1,0:T(8,128)(2,1)}, u32[]{:S(2)}) copy-start(bf16[8,128,128]{2,1,0:T(8,128)(2,1)} %copy-done.30) | copy-start | bytes 786436
  734.3 41.2 %copy-start.1 = (bf16[128,1024]{1,0:T(8,128)(2,1)S(1)}, bf16[128,1024]{1,0:T(8,128)(2,1)}, u32[]{:S(2)}) copy-start(bf16[128,1024]{1,0:T(8,128)(2,1)} %param.38) | copy-start | bytes 786436
  743.5 30.1 %all-to-all-start.4 = ((bf16[8,128,512]{2,1,0:T(8,128)(2,1)}), bf16[8,128,512]{2,1,0:T(8,128)(2,1)S(1)}, u32[]{:S(2)}, u32[]{:S(2)}) async-start(bf16[8,128,512]{2,1,0:T(8,128)(2,1)} %copy.305), calls=%async_computation.4 | async-start | bytes 2097152 | tf_op jit(solution)/shard_map/all_to_all | solution.py:203
  (8 other events, 11.1 us)
where the time goes:
time: 784 us; the launch traced here: 776 us
  starting transfers between devices  263 us (34%)
  local copies, waits for them, and re-layouts  168 us (21%)
  waiting for transfers between devices  139 us (18%)
  loops' own time  84.8 us (11%)
  matrix products  72.9 us (9%)
  other arithmetic  46.6 us (6%)
    ppermute x12, starting transfers between devices, from_behind(): return lax.ppermute(shard, axis, pairs)  212 us
    ppermute x12, waiting for transfers between devices, from_behind(): return lax.ppermute(shard, axis, pairs)  63.1 us
    another operation x4, loops' own time, on_device(): lax.fori_loop(0, count * count, grad_step, (grad_q, empty, empty))  42.6 us
    another operation x4, loops' own time, on_device(): forward = lax.fori_loop(0, count * count, fwd_step, forward)  40.7 us
    slice x64, local copies, waits for them, and re-layouts, tile_active(): return (k_pos[0] <= q_pos[-1]) & (k_pos[-1] >= jnp.min(q_start))  38.4 us
    dynamic_update_slice x6, local copies, waits for them, and re-layouts, fwd_work(): lax.dynamic_update_slice_in_dim(out_acc, new_out, q_first, 0)  32.9 us
    dynamic_update_slice x6, local copies, waits for them, and re-layouts, grad_work(): lax.dynamic_update_slice_in_dim(acc_q, lax.dynamic_slice_in_dim(acc_q, q_...  26.5 us
    all_to_all x1, starting transfers between devices, on_device(): lax.all_to_all(out_v, 'uly', split_axis=0, concat_axis=1, tiled=True)  26.3 us
  transfers between devices with their start and end apart: 19, of which 12 were waited for; matrix products, arithmetic and copies ran while one was open for 17% of the time, Pallas kernels for 0%

commit v1 on v0

v1 whole, which is shorter than its diff:
```python
import functools
import math

import jax
import jax.numpy as jnp
from jax import lax
from jax.experimental import pallas as pl
from jax.experimental.pallas import tpu as pltpu
from jax.sharding import PartitionSpec as P

HEAD_SIZE = 128
REACH = 3
Q_BLOCK = 256
K_BLOCK = 512

NEG = -1e30


def from_behind(shard, axis, by):
    length = lax.axis_size(axis)
    pairs = [(i, i + by) for i in range(length) if 0 <= i + by < length]
    return lax.ppermute(shard, axis, pairs)


def attention_kernel(
    meta_ref, q_ref, do_ref, k_ref, v_ref, qs_ref,
    dq_ref, dk_ref, dv_ref,
    m_s, l_s, acc_s, lse_s, delta_s, dq_s,
    *, groups, q_blocks, scale,
):
    T, TK, D = Q_BLOCK, K_BLOCK, HEAD_SIZE
    dk_ref[...] = jnp.zeros_like(dk_ref)
    dv_ref[...] = jnp.zeros_like(dv_ref)
    q_base = meta_ref[0]
    k_base = meta_ref[1]

    def tile_mask(q0, kb):
        q_pos = q_base + q0 + lax.broadcasted_iota(jnp.int32, (T, TK), 0)
        k_pos = k_base + kb * TK + lax.broadcasted_iota(jnp.int32, (T, TK), 1)
        start = qs_ref[pl.ds(q0, T), :]
        return (k_pos <= q_pos) & (k_pos >= start)

    def q_block(qb, carry):
        q0 = pl.multiple_of(qb * T, T)
        lo = meta_ref[2 + 2 * qb]
        hi = meta_ref[3 + 2 * qb]
        m_s[...] = jnp.full_like(m_s, NEG)
        l_s[...] = jnp.zeros_like(l_s)
        acc_s[...] = jnp.zeros_like(acc_s)

        def fwd(kb, c):
            k0 = pl.multiple_of(kb * TK, TK)
            k = k_ref[pl.ds(k0, TK), :]
            v = v_ref[pl.ds(k0, TK), :]
            mask = tile_mask(q0, kb)
            for h in range(groups):
                qh = q_ref[pl.ds(q0, T), pl.ds(h * D, D)]
                raw = lax.dot_general(
                    qh, k, (((1,), (1,)), ((), ())), preferred_element_type=jnp.float32
                ) * scale
                s = jnp.where(mask, raw, NEG)
                old_high = m_s[h]
                new_high = jnp.maximum(old_high, jnp.max(s, axis=1, keepdims=True))
                factor = jnp.exp(old_high - new_high)
                terms = jnp.where(mask, jnp.exp(s - new_high), 0.0)
                l_s[h] = l_s[h] * factor + jnp.sum(terms, axis=1, keepdims=True)
                acc_s[h] = acc_s[h] * factor + jnp.dot(
                    terms.astype(jnp.bfloat16), v, preferred_element_type=jnp.float32
                )
                m_s[h] = new_high
            return c

        lax.fori_loop(lo, hi, fwd, 0)
        for h in range(groups):
            total = l_s[h]
            lse_s[h] = m_s[h] + jnp.log(total)
            out = (acc_s[h] / total).astype(jnp.bfloat16).astype(jnp.float32)
            g = do_ref[pl.ds(q0, T), pl.ds(h * D, D)].astype(jnp.float32)
            delta_s[h] = jnp.sum(g * out, axis=1, keepdims=True)
        dq_s[...] = jnp.zeros_like(dq_s)

        def bwd(kb, c):
            k0 = pl.multiple_of(kb * TK, TK)
            k = k_ref[pl.ds(k0, TK), :]
            v = v_ref[pl.ds(k0, TK), :]
            mask = tile_mask(q0, kb)
            add_k = jnp.zeros((TK, D), jnp.float32)
            add_v = jnp.zeros((TK, D), jnp.float32)
            for h in range(groups):
                qh = q_ref[pl.ds(q0, T), pl.ds(h * D, D)]
                gh = do_ref[pl.ds(q0, T), pl.ds(h * D, D)]
                raw = lax.dot_general(
                    qh, k, (((1,), (1,)), ((), ())), preferred_element_type=jnp.float32
                ) * scale
                s = jnp.where(mask, raw, NEG)
                probs = jnp.where(mask, jnp.exp(s - lse_s[h]), 0.0)
                dprobs = lax.dot_general(
                    gh, v, (((1,), (1,)), ((), ())), preferred_element_type=jnp.float32
                )
                dscores = probs * (dprobs - delta_s[h])
                dq_s[h] = dq_s[h] + jnp.dot(
                    dscores.astype(jnp.bfloat16), k, preferred_element_type=jnp.float32
                )
                add_k = add_k + jnp.dot(
                    dscores.T.astype(jnp.bfloat16), qh, preferred_element_type=jnp.float32
                )
                add_v = add_v + jnp.dot(
                    probs.T.astype(jnp.bfloat16), gh, preferred_element_type=jnp.float32
                )
            dk_ref[pl.ds(k0, TK), :] = dk_ref[pl.ds(k0, TK), :] + add_k
            dv_ref[pl.ds(k0, TK), :] = dv_ref[pl.ds(k0, TK), :] + add_v
            return c

        lax.fori_loop(lo, hi, bwd, 0)
        for h in range(groups):
            dq_ref[pl.ds(q0, T), pl.ds(h * D, D)] = (scale * dq_s[h]).astype(dq_ref.dtype)
        return carry

    lax.fori_loop(0, q_blocks, q_block, 0)


def attend(meta, queries, gradient, key_window, value_window, q_start, groups, scale):
    rows = queries.shape[0]
    width = key_window.shape[0]
    q_blocks = rows // Q_BLOCK
    vmem = pltpu.MemorySpace.VMEM
    kernel = functools.partial(
        attention_kernel, groups=groups, q_blocks=q_blocks, scale=scale
    )
    return pl.pallas_call(
        kernel,
        out_shape=(
            jax.ShapeDtypeStruct(queries.shape, jnp.bfloat16),
            jax.ShapeDtypeStruct((width, HEAD_SIZE), jnp.float32),
            jax.ShapeDtypeStruct((width, HEAD_SIZE), jnp.float32),
        ),
        in_specs=[pl.BlockSpec(memory_space=pltpu.MemorySpace.SMEM)]
        + [pl.BlockSpec(memory_space=vmem)] * 5,
        out_specs=[pl.BlockSpec(memory_space=vmem)] * 3,
        scratch_shapes=[
            pltpu.VMEM((groups, Q_BLOCK, 1), jnp.float32),
            pltpu.VMEM((groups, Q_BLOCK, 1), jnp.float32),
            pltpu.VMEM((groups, Q_BLOCK, HEAD_SIZE), jnp.float32),
            pltpu.VMEM((groups, Q_BLOCK, 1), jnp.float32),
            pltpu.VMEM((groups, Q_BLOCK, 1), jnp.float32),
            pltpu.VMEM((groups, Q_BLOCK, HEAD_SIZE), jnp.float32),
        ],
        compiler_params=pltpu.CompilerParams(vmem_limit_bytes=48 * 1024 * 1024),
    )(meta, queries, gradient, key_window, value_window, q_start)


def on_device(queries, keys, values, output_gradient, doc_lengths):
    uly = lax.axis_size("uly")
    tokens = queries.shape[0]
    q_cols = queries.shape[1] // uly
    kv_cols = keys.shape[1] // uly
    packed = jnp.concatenate(
        [
            queries.reshape(tokens, uly, q_cols),
            output_gradient.reshape(tokens, uly, q_cols),
            keys.reshape(tokens, uly, kv_cols),
            values.reshape(tokens, uly, kv_cols),
        ],
        axis=2,
    )
    packed = lax.all_to_all(packed, "uly", split_axis=1, concat_axis=0, tiled=True)
    rows = packed.shape[0]
    packed = packed.reshape(rows, 2 * q_cols + 2 * kv_cols)
    queries = packed[:, :q_cols]
    gradient = packed[:, q_cols : 2 * q_cols]
    kv = packed[:, 2 * q_cols :]
    groups = q_cols // HEAD_SIZE
    softmax_scale = 1.0 / math.sqrt(HEAD_SIZE)

    window = [kv]
    for step in range(1, REACH + 1):
        window.append(from_behind(kv, "ctx", step))
    window = jnp.concatenate(window[::-1], axis=0)
    key_window = window[:, :HEAD_SIZE]
    value_window = window[:, HEAD_SIZE:]

    ctx_index = lax.axis_index("ctx")
    q_base = ctx_index * rows
    k_base = (ctx_index - REACH) * rows
    q_pos = q_base + jnp.arange(rows, dtype=jnp.int32)
    ends = jnp.cumsum(doc_lengths)
    q_start = jnp.sum(
        jnp.where(ends[None, :] <= q_pos[:, None], doc_lengths[None, :], 0), axis=1
    ).astype(jnp.int32)
    first_rows = jnp.arange(0, rows, Q_BLOCK, dtype=jnp.int32)
    lo = jnp.maximum((q_start[first_rows] - k_base) // K_BLOCK, 0)
    hi = (q_base + first_rows + Q_BLOCK - 1 - k_base) // K_BLOCK + 1
    meta = jnp.concatenate(
        [jnp.stack([q_base, k_base]).astype(jnp.int32), jnp.stack([lo, hi], axis=1).reshape(-1)]
    ).astype(jnp.int32)

    dq, dk_window, dv_window = attend(
        meta, queries, gradient, key_window, value_window, q_start[:, None], groups, softmax_scale
    )
    partials = jnp.concatenate([dk_window, dv_window], axis=1)
    total = partials[REACH * rows :]
    for step in range(1, REACH + 1):
        piece = partials[(REACH - step) * rows : (REACH - step + 1) * rows]
        total = total + from_behind(piece.astype(jnp.bfloat16), "ctx", -step).astype(jnp.float32)
    out_k = (softmax_scale * total[:, :HEAD_SIZE]).astype(jnp.bfloat16)
    out_v = total[:, HEAD_SIZE:].astype(jnp.bfloat16)
    result = jnp.concatenate([dq, out_k, out_v], axis=1)
    result = lax.all_to_all(result, "uly", split_axis=0, concat_axis=1, tiled=True)
    piece_cols = q_cols + 2 * kv_cols
    result = result.reshape(result.shape[0], uly, piece_cols)
    return (
        result[:, :, :q_cols].reshape(result.shape[0], uly * q_cols),
        result[:, :, q_cols : q_cols + kv_cols].reshape(result.shape[0], uly * kv_cols),
        result[:, :, q_cols + kv_cols :].reshape(result.shape[0], uly * kv_cols),
    )


def solution(mesh):
    return jax.shard_map(
        on_device,
        mesh=mesh,
        in_specs=(
            P(("ctx", "uly"), None),
            P(("ctx", "uly"), None),
            P(("ctx", "uly"), None),
            P(("ctx", "uly"), None),
            P(),
        ),
        out_specs=(P(("ctx", "uly"), None), P(("ctx", "uly"), None), P(("ctx", "uly"), None)),
        check_vma=False,
    )
```

time: 784 us -> 367 us (0.47)
  the two profiles are of different devices: /device:TPU:22 before, /device:TPU:14 now
where the time goes in v1:
time: 367 us; the launch traced here: 360 us
  waiting for transfers between devices  168 us (46%)
  starting transfers between devices  60.2 us (16%)
  Pallas kernels  57.8 us (16%)
  blocking collectives  57.4 us (16%)
  local copies, waits for them, and re-layouts  11.4 us (3%)
  other arithmetic  4.31 us (1%)
    ppermute x6, waiting for transfers between devices, from_behind(): return lax.ppermute(shard, axis, pairs)  109 us
    all_to_all x1, waiting for transfers between devices, on_device(): lax.all_to_all(packed, 'uly', split_axis=1, concat_axis=0, tiled=True)  59.3 us
    pallas_call x1, Pallas kernels, attend(): pl.pallas_call(kernel, out_shape=(jax.ShapeDtypeStruct(queries.shape, jnp...  57.8 us
    all_to_all x1, blocking collectives, on_device(): lax.all_to_all(result, 'uly', split_axis=0, concat_axis=1, tiled=True)  57.4 us
    ppermute x6, starting transfers between devices, from_behind(): return lax.ppermute(shard, axis, pairs)  54.2 us
  transfers between devices with their start and end apart: 7, of which 7 were waited for; matrix products, arithmetic and copies ran while one was open for 0% of the time, Pallas kernels for 0%

profile of v1, /device:TPU:14, one launch (start us, length us, event | category | flops | bytes accessed | tf_op | source)
XLA Modules:
  0.0 360.4 jit_solution(11894741976688956878)
XLA Ops:
  0.6 0.0 copy-start
  0.6 0.9 copy-done
  1.6 1.1 copy_bitcast_fusion.4
  2.7 1.8 copy_bitcast_fusion
  4.4 1.6 pad_maximum_fusion
  6.1 0.0 copy-start.2
  6.1 6.0 %all-to-all-start = ((bf16[128,8,1280]{2,0,1:T(8,128)(2,1)}), bf16[128,8,1280]{2,0,1:T(8,128)(2,1)S(1)}, u32[]{:S(2)}, u32[]{:S(2)}) async-start(bf16[128,8,1280]{2,0,1:T(8,128)(2,1)} %pad_maximum_fusion), calls=%async_computation | async-start | bytes 5242880 | tf_op jit(solution)/shard_map/all_to_all | solution.py:166
  12.1 0.0 copy-done.2
  12.1 0.1 copy.27
  12.2 0.1 reduce-window.8
  12.3 0.1 reduce
  12.4 0.1 select_reduce_fusion
  12.5 0.6 gather_fusion
  13.2 59.3 %all-to-all-done = bf16[128,8,1280]{2,0,1:T(8,128)(2,1)S(1)} async-done(((bf16[128,8,1280]{2,0,1:T(8,128)(2,1)}), bf16[128,8,1280]{2,0,1:T(8,128)(2,1)S(1)}, u32[]{:S(2)}, u32[]{:S(2)}) %all-to-all-start) | async-done | bytes 2621472 | tf_op jit(solution)/shard_map/all_to_all | solution.py:166
  72.4 0.8 slice.64
  73.2 6.7 %collective-permute-start.2 = (bf16[1024,256]{1,0:T(8,128)(2,1)}, bf16[1024,256]{1,0:T(8,128)(2,1)}, u32[]{:S(2)}, u32[]{:S(2)}) collective-permute-start(bf16[1024,256]{1,0:T(8,128)(2,1)} %slice.64), channel_id=1, source_target_pairs={{0,8},{8,16},{16,24},{24,32},{32,40},{40,48},{48,56},{56,64},{64,7... | collective-permute-start | bytes 1572872 | tf_op jit(solution)/shard_map/ppermute | solution.py:22
  79.9 4.3 %collective-permute-start.1 = (bf16[1024,256]{1,0:T(8,128)(2,1)}, bf16[1024,256]{1,0:T(8,128)(2,1)}, u32[]{:S(2)}, u32[]{:S(2)}) collective-permute-start(bf16[1024,256]{1,0:T(8,128)(2,1)} %slice.64), channel_id=1, source_target_pairs={{0,16},{8,24},{16,32},{24,40},{32,48},{40,56},{48,64},{56,72},{64,... | collective-permute-start | bytes 1572872 | tf_op jit(solution)/shard_map/ppermute | solution.py:22
  84.2 3.4 collective-permute-start
  87.7 0.1 copy.28
  87.7 0.1 reshape.201
  87.8 0.2 copy.33.qs_ref
  88.1 0.1 pad_add_fusion.1.meta_ref
  88.1 0.1 fusion.6
  88.3 51.9 %collective-permute-done.2 = bf16[1024,256]{1,0:T(8,128)(2,1)} collective-permute-done((bf16[1024,256]{1,0:T(8,128)(2,1)}, bf16[1024,256]{1,0:T(8,128)(2,1)}, u32[]{:S(2)}, u32[]{:S(2)}) %collective-permute-start.2) | collective-permute-done | bytes 524320 | tf_op jit(solution)/shard_map/ppermute | solution.py:22
  140.2 18.8 %collective-permute-done.1 = bf16[1024,256]{1,0:T(8,128)(2,1)} collective-permute-done((bf16[1024,256]{1,0:T(8,128)(2,1)}, bf16[1024,256]{1,0:T(8,128)(2,1)}, u32[]{:S(2)}, u32[]{:S(2)}) %collective-permute-start.1) | collective-permute-done | bytes 524320 | tf_op jit(solution)/shard_map/ppermute | solution.py:22
  159.0 11.1 %collective-permute-done = bf16[1024,256]{1,0:T(8,128)(2,1)} collective-permute-done((bf16[1024,256]{1,0:T(8,128)(2,1)}, bf16[1024,256]{1,0:T(8,128)(2,1)}, u32[]{:S(2)}, u32[]{:S(2)}) %collective-permute-start) | collective-permute-done | bytes 524320 | tf_op jit(solution)/shard_map/ppermute | solution.py:22
  170.1 1.7 pad_maximum_fusion.1
  171.8 0.1 fusion.8
  171.9 57.8 %shard_map.76 = (bf16[1024,512]{1,0:T(8,128)(2,1)S(1)}, f32[4096,128]{1,0:T(8,128)}, f32[4096,128]{1,0:T(8,128)}) custom-call(s32[10]{0:T(128)S(1)} %pad_add_fusion.1.meta_ref, bf16[1024,512]{1,0:T(8,128)(2,1)S(1)} %get-tuple-element.10.q_ref, bf16[1024,512]{1,0:T(8,128)(2,1)S(1)} %get-tuple-element.9.do_ref, bf16[4096,128]{1,0:T(8,128)(2,1)S(1)} %get-tuple-element.15.k_ref, ...), custom_call_target="tpu_custom_call" | custom-call | tf_op jit(solution)/shard_map/pallas_call | solution.py:130
  229.8 0.0 copy-start.1
  229.8 1.9 constant_dynamic-update-slice_fusion.1
  231.7 0.3 copy-done.1
  232.0 0.2 constant_dynamic-update-slice_fusion
  232.1 0.2 convert.8
  232.4 0.1 fusion.7
  232.5 36.0 %collective-permute-start.3 = (bf16[1024,256]{1,0:T(8,128)(2,1)S(1)}, bf16[1024,256]{1,0:T(8,128)(2,1)S(1)}, u32[]{:S(2)}, u32[]{:S(2)}) collective-permute-start(bf16[1024,256]{1,0:T(8,128)(2,1)S(1)} %get-tuple-element.11), channel_id=1, source_target_pairs={{8,0},{16,8},{24,16},{32,24},{40,32},{48,40},{56,48},{64,56},{72,6... | collective-permute-start | bytes 1572872 | tf_op jit(solution)/shard_map/ppermute | solution.py:22
  268.5 1.9 collective-permute-start.5
  270.4 1.9 collective-permute-start.4
  272.3 8.5 %collective-permute-done.3 = bf16[1024,256]{1,0:T(8,128)(2,1)S(1)} collective-permute-done((bf16[1024,256]{1,0:T(8,128)(2,1)S(1)}, bf16[1024,256]{1,0:T(8,128)(2,1)S(1)}, u32[]{:S(2)}, u32[]{:S(2)}) %collective-permute-start.3) | collective-permute-done | bytes 524320 | tf_op jit(solution)/shard_map/ppermute | solution.py:22
  280.8 13.0 %collective-permute-done.5 = bf16[1024,256]{1,0:T(8,128)(2,1)S(1)} collective-permute-done((bf16[1024,256]{1,0:T(8,128)(2,1)S(1)}, bf16[1024,256]{1,0:T(8,128)(2,1)S(1)}, u32[]{:S(2)}, u32[]{:S(2)}) %collective-permute-start.5) | collective-permute-done | bytes 524320 | tf_op jit(solution)/shard_map/ppermute | solution.py:22
  293.8 5.9 %collective-permute-done.4 = bf16[1024,256]{1,0:T(8,128)(2,1)S(1)} collective-permute-done((bf16[1024,256]{1,0:T(8,128)(2,1)S(1)}, bf16[1024,256]{1,0:T(8,128)(2,1)S(1)}, u32[]{:S(2)}, u32[]{:S(2)}) %collective-permute-start.4) | collective-permute-done | bytes 524320 | tf_op jit(solution)/shard_map/ppermute | solution.py:22
  299.7 0.2 fusion.1
  300.1 0.1 pad_maximum_fusion.2
  300.2 57.4 %all_to_all.31 = bf16[8,128,768]{2,1,0:T(8,128)(2,1)S(1)} all-to-all(bf16[8,128,768]{2,1,0:T(8,128)(2,1)S(1)} %bitcast.57), channel_id=1, replica_groups=mesh['ctx'=32,'uly'=8] {'uly'}, dimensions={0} | all-to-all | bytes 3145728 | tf_op jit(solution)/shard_map/all_to_all | solution.py:208
  357.6 0.1 slice_bitcast_fusion.1
  357.7 0.1 slice_bitcast_fusion
  357.8 1.1 copy.41
  358.9 0.8 copy.50
  359.6 0.8 copy.51
  (7 shorter events, 0.1 us)
Async XLA Ops:
  0.6 1.0 copy-start
  6.1 6.0 %copy-start.2 = (s32[32]{0:T(128)S(1)}, s32[32]{0:T(128)}, u32[]{:S(2)}) copy-start(s32[32]{0:T(128)} %param.9) | copy-start | bytes 388
  6.1 66.3 %all-to-all-start = ((bf16[128,8,1280]{2,0,1:T(8,128)(2,1)}), bf16[128,8,1280]{2,0,1:T(8,128)(2,1)S(1)}, u32[]{:S(2)}, u32[]{:S(2)}) async-start(bf16[128,8,1280]{2,0,1:T(8,128)(2,1)} %pad_maximum_fusion), calls=%async_computation | async-start | bytes 5242880 | tf_op jit(solution)/shard_map/all_to_all | solution.py:166
  73.2 66.9 %collective-permute-start.2 = (bf16[1024,256]{1,0:T(8,128)(2,1)}, bf16[1024,256]{1,0:T(8,128)(2,1)}, u32[]{:S(2)}, u32[]{:S(2)}) collective-permute-start(bf16[1024,256]{1,0:T(8,128)(2,1)} %slice.64), channel_id=1, source_target_pairs={{0,8},{8,16},{16,24},{24,32},{32,40},{40,48},{48,56},{56,64},{64,7... | collective-permute-start | bytes 1572872 | tf_op jit(solution)/shard_map/ppermute | solution.py:22
  79.9 79.1 %collective-permute-start.1 = (bf16[1024,256]{1,0:T(8,128)(2,1)}, bf16[1024,256]{1,0:T(8,128)(2,1)}, u32[]{:S(2)}, u32[]{:S(2)}) collective-permute-start(bf16[1024,256]{1,0:T(8,128)(2,1)} %slice.64), channel_id=1, source_target_pairs={{0,16},{8,24},{16,32},{24,40},{32,48},{40,56},{48,64},{56,72},{64,... | collective-permute-start | bytes 1572872 | tf_op jit(solution)/shard_map/ppermute | solution.py:22
  84.2 85.9 %collective-permute-start = (bf16[1024,256]{1,0:T(8,128)(2,1)}, bf16[1024,256]{1,0:T(8,128)(2,1)}, u32[]{:S(2)}, u32[]{:S(2)}) collective-permute-start(bf16[1024,256]{1,0:T(8,128)(2,1)} %slice.64), channel_id=1, source_target_pairs={{0,24},{8,32},{16,40},{24,48},{32,56},{40,64},{48,72},{56,80},{64,... | collective-permute-start | bytes 1572872 | tf_op jit(solution)/shard_map/ppermute | solution.py:22
  229.8 2.2 copy-start.1
  232.5 48.4 %collective-permute-start.3 = (bf16[1024,256]{1,0:T(8,128)(2,1)S(1)}, bf16[1024,256]{1,0:T(8,128)(2,1)S(1)}, u32[]{:S(2)}, u32[]{:S(2)}) collective-permute-start(bf16[1024,256]{1,0:T(8,128)(2,1)S(1)} %get-tuple-element.11), channel_id=1, source_target_pairs={{8,0},{16,8},{24,16},{32,24},{40,32},{48,40},{56,48},{64,56},{72,6... | collective-permute-start | bytes 1572872 | tf_op jit(solution)/shard_map/ppermute | solution.py:22
  268.5 25.3 %collective-permute-start.5 = (bf16[1024,256]{1,0:T(8,128)(2,1)S(1)}, bf16[1024,256]{1,0:T(8,128)(2,1)S(1)}, u32[]{:S(2)}, u32[]{:S(2)}) collective-permute-start(bf16[1024,256]{1,0:T(8,128)(2,1)S(1)} %get-tuple-element.12), channel_id=1, source_target_pairs={{24,0},{32,8},{40,16},{48,24},{56,32},{64,40},{72,48},{80,56},{88,... | collective-permute-start | bytes 1572872 | tf_op jit(solution)/shard_map/ppermute | solution.py:22
  270.4 29.3 %collective-permute-start.4 = (bf16[1024,256]{1,0:T(8,128)(2,1)S(1)}, bf16[1024,256]{1,0:T(8,128)(2,1)S(1)}, u32[]{:S(2)}, u32[]{:S(2)}) collective-permute-start(bf16[1024,256]{1,0:T(8,128)(2,1)S(1)} %get-tuple-element.13), channel_id=1, source_target_pairs={{16,0},{24,8},{32,16},{40,24},{48,32},{56,40},{64,48},{72,56},{80,... | collective-permute-start | bytes 1572872 | tf_op jit(solution)/shard_map/ppermute | solution.py:22

commit v2 on v1

--- a/solution.py
+++ b/solution.py
@@ -16,10 +16,30 @@
 NEG = -1e30
 
 
-def from_behind(shard, axis, by):
-    length = lax.axis_size(axis)
-    pairs = [(i, i + by) for i in range(length) if 0 <= i + by < length]
-    return lax.ppermute(shard, axis, pairs)
+def mirror_of(uly, cores):
+    run = uly // cores
+    return [(run - 1 - u // cores) * cores + u % cores for u in range(uly)]
+
+
+def from_behind(shard, by, flips, cores):
+    ctx = lax.axis_size("ctx")
+    uly = lax.axis_size("uly")
+    mirror = mirror_of(uly, cores)
+    pairs = []
+    for c in range(ctx):
+        d = c + by
+        if not 0 <= d < ctx:
+            continue
+        for u in range(uly):
+            group = mirror[u] if flips[c] else u
+            pairs.append((c * uly + u, d * uly + (mirror[group] if flips[d] else group)))
+    return lax.ppermute(shard, ("ctx", "uly"), pairs)
+
+
+def mirrored(x, flip, cores):
+    rows, uly = x.shape[0], x.shape[1]
+    split = x.reshape(rows, uly // cores, cores, x.shape[2])
+    return jnp.where(flip, split[:, ::-1], split).reshape(x.shape)
 
 
 def attention_kernel(
@@ -149,8 +169,10 @@
     )(meta, queries, gradient, key_window, value_window, q_start)
 
 
-def on_device(queries, keys, values, output_gradient, doc_lengths):
+def on_device(queries, keys, values, output_gradient, doc_lengths, flips, cores):
     uly = lax.axis_size("uly")
+    ctx_index = lax.axis_index("ctx")
+    flip = jnp.asarray(flips)[ctx_index]
     tokens = queries.shape[0]
     q_cols = queries.shape[1] // uly
     kv_cols = keys.shape[1] // uly
@@ -163,6 +185,7 @@
         ],
         axis=2,
     )
+    packed = mirrored(packed, flip, cores)
     packed = lax.all_to_all(packed, "uly", split_axis=1, concat_axis=0, tiled=True)
     rows = packed.shape[0]
     packed = packed.reshape(rows, 2 * q_cols + 2 * kv_cols)
@@ -174,12 +197,11 @@
 
     window = [kv]
     for step in range(1, REACH + 1):
-        window.append(from_behind(kv, "ctx", step))
+        window.append(from_behind(kv, step, flips, cores))
     window = jnp.concatenate(window[::-1], axis=0)
     key_window = window[:, :HEAD_SIZE]
     value_window = window[:, HEAD_SIZE:]
 
-    ctx_index = lax.axis_index("ctx")
     q_base = ctx_index * rows
     k_base = (ctx_index - REACH) * rows
     q_pos = q_base + jnp.arange(rows, dtype=jnp.int32)
@@ -201,13 +223,13 @@
     total = partials[REACH * rows :]
     for step in range(1, REACH + 1):
         piece = partials[(REACH - step) * rows : (REACH - step + 1) * rows]
-        total = total + from_behind(piece.astype(jnp.bfloat16), "ctx", -step).astype(jnp.float32)
+        total = total + from_behind(piece.astype(jnp.bfloat16), -step, flips, cores).astype(jnp.float32)
     out_k = (softmax_scale * total[:, :HEAD_SIZE]).astype(jnp.bfloat16)
     out_v = total[:, HEAD_SIZE:].astype(jnp.bfloat16)
     result = jnp.concatenate([dq, out_k, out_v], axis=1)
     result = lax.all_to_all(result, "uly", split_axis=0, concat_axis=1, tiled=True)
     piece_cols = q_cols + 2 * kv_cols
-    result = result.reshape(result.shape[0], uly, piece_cols)
+    result = mirrored(result.reshape(result.shape[0], uly, piece_cols), flip, cores)
     return (
         result[:, :, :q_cols].reshape(result.shape[0], uly * q_cols),
         result[:, :, q_cols : q_cols + kv_cols].reshape(result.shape[0], uly * kv_cols),
@@ -215,9 +237,20 @@
     )
 
 
+def layout_of(mesh):
+    devices = mesh.devices
+    cores = len({getattr(d, "core_on_chip", 0) for d in devices.flat})
+    run = devices.shape[1] // cores
+    coords = [getattr(devices[c, 0], "coords", None) for c in range(devices.shape[0])]
+    if any(xyz is None for xyz in coords):
+        return (False,) * devices.shape[0], cores
+    return tuple(bool((xyz[2] // run) % 2) for xyz in coords), cores
+
+
 def solution(mesh):
+    flips, cores = layout_of(mesh)
     return jax.shard_map(
-        on_device,
+        functools.partial(on_device, flips=flips, cores=cores),
         mesh=mesh,
         in_specs=(
             P(("ctx", "uly"), None),

time: 367 us -> 377 us (1.027)
  the two profiles are of different devices: /device:TPU:14 before, /device:TPU:10 now
where the time goes in v2:
time: 377 us; the launch traced here: 383 us
  waiting for transfers between devices  203 us (54%)
  starting transfers between devices  57.5 us (15%)
  Pallas kernels  53.1 us (14%)
  blocking collectives  41.2 us (11%)
  local copies, waits for them, and re-layouts  21.5 us (6%)
  other arithmetic  6.77 us (2%)
    ppermute x6, waiting for transfers between devices, from_behind(): return lax.ppermute(shard, ('ctx', 'uly'), pairs)  143 us
    all_to_all x1, waiting for transfers between devices, on_device(): lax.all_to_all(packed, 'uly', split_axis=1, concat_axis=0, tiled=True)  59.3 us
    pallas_call x1, Pallas kernels, attend(): pl.pallas_call(kernel, out_shape=(jax.ShapeDtypeStruct(queries.shape, jnp...  53.1 us
    ppermute x6, starting transfers between devices, from_behind(): return lax.ppermute(shard, ('ctx', 'uly'), pairs)  51.5 us
    all_to_all x1, blocking collectives, on_device(): lax.all_to_all(result, 'uly', split_axis=0, concat_axis=1, tiled=True)  41.2 us
  transfers between devices with their start and end apart: 7, of which 5 were waited for; matrix products, arithmetic and copies ran while one was open for 0% of the time, Pallas kernels for 0%

profile of v2, /device:TPU:10, one launch (start us, length us, event | category | flops | bytes accessed | tf_op | source)
XLA Modules:
  0.0 383.5 jit_solution(2574957262238128553)
XLA Ops:
  0.6 0.0 copy-start.1
  0.6 1.2 concatenate.27
  1.9 1.1 concatenate.28
  3.0 2.6 concatenate.25
  5.6 0.0 copy-done.1
  5.6 0.0 copy-start.3
  5.6 1.6 concatenate.26
  7.2 1.9 constant_dynamic-update-slice_fusion.3
  9.1 0.0 copy-done.3
  9.1 0.6 dynamic_slice.3
  9.7 2.1 constant_dynamic-update-slice_fusion.2
  11.8 0.4 constant_dynamic-update-slice_fusion.1
  12.2 0.4 constant_dynamic-update-slice_fusion
  12.6 3.3 broadcast_select_fusion
  15.8 2.0 copy.20
  17.8 0.0 copy-start.2
  17.8 6.0 %all-to-all-start = ((bf16[128,8,1280]{2,0,1:T(8,128)(2,1)}), bf16[128,8,1280]{2,0,1:T(8,128)(2,1)S(1)}, u32[]{:S(2)}, u32[]{:S(2)}) async-start(bf16[128,8,1280]{2,0,1:T(8,128)(2,1)} %bitcast.44), calls=%async_computation | async-start | bytes 5242880 | tf_op jit(solution)/shard_map/all_to_all | solution.py:189
  23.9 0.0 copy-done.2
  23.9 0.1 copy.18
  23.9 0.1 reduce-window.8
  24.0 0.1 reduce
  24.2 0.1 select_reduce_fusion
  24.2 0.6 gather_fusion
  24.9 59.3 %all-to-all-done = bf16[128,8,1280]{2,0,1:T(8,128)(2,1)S(1)} async-done(((bf16[128,8,1280]{2,0,1:T(8,128)(2,1)}), bf16[128,8,1280]{2,0,1:T(8,128)(2,1)S(1)}, u32[]{:S(2)}, u32[]{:S(2)}) %all-to-all-start) | async-done | bytes 2621472 | tf_op jit(solution)/shard_map/all_to_all | solution.py:189
  84.2 0.8 slice.64
  85.0 3.4 collective-permute-start.2
  88.4 5.3 %collective-permute-start.1 = (bf16[1024,256]{1,0:T(8,128)(2,1)}, bf16[1024,256]{1,0:T(8,128)(2,1)}, u32[]{:S(2)}, u32[]{:S(2)}) collective-permute-start(bf16[1024,256]{1,0:T(8,128)(2,1)} %slice.64), channel_id=1, source_target_pairs={{0,16},{1,17},{2,18},{3,19},{4,20},{5,21},{6,22},{7,23},{8,24},{9,... | collective-permute-start | bytes 1572872 | tf_op jit(solution)/shard_map/ppermute | solution.py:36
  93.7 4.2 %collective-permute-start = (bf16[1024,256]{1,0:T(8,128)(2,1)}, bf16[1024,256]{1,0:T(8,128)(2,1)}, u32[]{:S(2)}, u32[]{:S(2)}) collective-permute-start(bf16[1024,256]{1,0:T(8,128)(2,1)} %slice.64), channel_id=1, source_target_pairs={{0,24},{1,25},{2,26},{3,27},{4,28},{5,29},{6,30},{7,31},{8,38},{9,... | collective-permute-start | bytes 1572872 | tf_op jit(solution)/shard_map/ppermute | solution.py:36
  97.9 0.1 copy.19
  98.0 0.1 reshape.207
  98.1 0.2 copy.21.qs_ref
  98.3 0.1 pad_add_fusion.1.meta_ref
  98.4 0.2 fusion.6
  98.6 3.4 collective-permute-done.2
  102.0 49.7 %collective-permute-done.1 = bf16[1024,256]{1,0:T(8,128)(2,1)} collective-permute-done((bf16[1024,256]{1,0:T(8,128)(2,1)}, bf16[1024,256]{1,0:T(8,128)(2,1)}, u32[]{:S(2)}, u32[]{:S(2)}) %collective-permute-start.1) | collective-permute-done | bytes 524320 | tf_op jit(solution)/shard_map/ppermute | solution.py:36
  151.7 0.0 collective-permute-done
  151.8 1.7 pad_maximum_fusion
  153.4 0.1 fusion.8
  153.6 53.1 %shard_map.85 = (bf16[1024,512]{1,0:T(8,128)(2,1)S(1)}, f32[4096,128]{1,0:T(8,128)}, f32[4096,128]{1,0:T(8,128)}) custom-call(s32[10]{0:T(128)S(1)} %pad_add_fusion.1.meta_ref, bf16[1024,512]{1,0:T(8,128)(2,1)S(1)} %get-tuple-element.10.q_ref, bf16[1024,512]{1,0:T(8,128)(2,1)S(1)} %get-tuple-element.9.do_ref, bf16[4096,128]{1,0:T(8,128)(2,1)S(1)} %get-tuple-element.15.k_ref, ...), custom_call_target="tpu_custom_call" | custom-call | tf_op jit(solution)/shard_map/pallas_call | solution.py:150
  206.6 0.0 copy-start
  206.6 1.9 constant_dynamic-update-slice_fusion.5
  208.5 0.3 copy-done
  208.8 0.2 constant_dynamic-update-slice_fusion.4
  209.0 0.2 convert.8
  209.2 0.1 fusion.7
  209.3 1.9 collective-permute-start.3
  211.3 33.3 %collective-permute-start.5 = (bf16[1024,256]{1,0:T(8,128)(2,1)S(1)}, bf16[1024,256]{1,0:T(8,128)(2,1)S(1)}, u32[]{:S(2)}, u32[]{:S(2)}) collective-permute-start(bf16[1024,256]{1,0:T(8,128)(2,1)S(1)} %get-tuple-element.12), channel_id=1, source_target_pairs={{24,0},{25,1},{26,2},{27,3},{28,4},{29,5},{30,6},{31,7},{32,14},{3... | collective-permute-start | bytes 1572872 | tf_op jit(solution)/shard_map/ppermute | solution.py:36
  244.5 3.4 collective-permute-start.4
  247.9 25.0 %collective-permute-done.3 = bf16[1024,256]{1,0:T(8,128)(2,1)S(1)} collective-permute-done((bf16[1024,256]{1,0:T(8,128)(2,1)S(1)}, bf16[1024,256]{1,0:T(8,128)(2,1)S(1)}, u32[]{:S(2)}, u32[]{:S(2)}) %collective-permute-start.3) | collective-permute-done | bytes 524320 | tf_op jit(solution)/shard_map/ppermute | solution.py:36
  272.9 65.1 %collective-permute-done.5 = bf16[1024,256]{1,0:T(8,128)(2,1)S(1)} collective-permute-done((bf16[1024,256]{1,0:T(8,128)(2,1)S(1)}, bf16[1024,256]{1,0:T(8,128)(2,1)S(1)}, u32[]{:S(2)}, u32[]{:S(2)}) %collective-permute-start.5) | collective-permute-done | bytes 524320 | tf_op jit(solution)/shard_map/ppermute | solution.py:36
  338.1 0.0 collective-permute-done.4
  338.1 0.2 fusion.1
  338.4 0.1 pad_maximum_fusion.1
  338.5 41.2 %all_to_all.31 = bf16[8,128,768]{2,1,0:T(8,128)(2,1)S(1)} all-to-all(bf16[8,128,768]{2,1,0:T(8,128)(2,1)S(1)} %bitcast.45), channel_id=1, replica_groups=mesh['ctx'=32,'uly'=8] {'uly'}, dimensions={0} | all-to-all | bytes 3145728 | tf_op jit(solution)/shard_map/all_to_all | solution.py:230
  379.8 0.9 reverse_select_fusion
  380.6 0.1 slice_bitcast_fusion.1
  380.8 0.1 slice_bitcast_fusion
  380.9 1.1 copy.27
  381.9 0.8 copy.32
  382.7 0.8 copy.33
  (7 shorter events, 0.1 us)
Async XLA Ops:
  0.6 5.0 %copy-start.1 = (bf16[128,4096]{1,0:T(8,128)(2,1)S(1)}, bf16[128,4096]{1,0:T(8,128)(2,1)}, u32[]{:S(2)}) copy-start(bf16[128,4096]{1,0:T(8,128)(2,1)} %param.9) | copy-start | bytes 3145732
  5.6 3.5 copy-start.3
  17.8 6.0 %copy-start.2 = (s32[32]{0:T(128)S(1)}, s32[32]{0:T(128)}, u32[]{:S(2)}) copy-start(s32[32]{0:T(128)} %param.10) | copy-start | bytes 388
  17.8 66.3 %all-to-all-start = ((bf16[128,8,1280]{2,0,1:T(8,128)(2,1)}), bf16[128,8,1280]{2,0,1:T(8,128)(2,1)S(1)}, u32[]{:S(2)}, u32[]{:S(2)}) async-start(bf16[128,8,1280]{2,0,1:T(8,128)(2,1)} %bitcast.44), calls=%async_computation | async-start | bytes 5242880 | tf_op jit(solution)/shard_map/all_to_all | solution.py:189
  85.0 17.0 %collective-permute-start.2 = (bf16[1024,256]{1,0:T(8,128)(2,1)}, bf16[1024,256]{1,0:T(8,128)(2,1)}, u32[]{:S(2)}, u32[]{:S(2)}) collective-permute-start(bf16[1024,256]{1,0:T(8,128)(2,1)} %slice.64), channel_id=1, source_target_pairs={{0,8},{1,9},{2,10},{3,11},{4,12},{5,13},{6,14},{7,15},{8,16},{9,17... | collective-permute-start | bytes 1572872 | tf_op jit(solution)/shard_map/ppermute | solution.py:36
  88.4 63.4 %collective-permute-start.1 = (bf16[1024,256]{1,0:T(8,128)(2,1)}, bf16[1024,256]{1,0:T(8,128)(2,1)}, u32[]{:S(2)}, u32[]{:S(2)}) collective-permute-start(bf16[1024,256]{1,0:T(8,128)(2,1)} %slice.64), channel_id=1, source_target_pairs={{0,16},{1,17},{2,18},{3,19},{4,20},{5,21},{6,22},{7,23},{8,24},{9,... | collective-permute-start | bytes 1572872 | tf_op jit(solution)/shard_map/ppermute | solution.py:36
  93.7 58.1 %collective-permute-start = (bf16[1024,256]{1,0:T(8,128)(2,1)}, bf16[1024,256]{1,0:T(8,128)(2,1)}, u32[]{:S(2)}, u32[]{:S(2)}) collective-permute-start(bf16[1024,256]{1,0:T(8,128)(2,1)} %slice.64), channel_id=1, source_target_pairs={{0,24},{1,25},{2,26},{3,27},{4,28},{5,29},{6,30},{7,31},{8,38},{9,... | collective-permute-start | bytes 1572872 | tf_op jit(solution)/shard_map/ppermute | solution.py:36
  206.6 2.2 copy-start
  209.3 63.6 %collective-permute-start.3 = (bf16[1024,256]{1,0:T(8,128)(2,1)S(1)}, bf16[1024,256]{1,0:T(8,128)(2,1)S(1)}, u32[]{:S(2)}, u32[]{:S(2)}) collective-permute-start(bf16[1024,256]{1,0:T(8,128)(2,1)S(1)} %get-tuple-element.11), channel_id=1, source_target_pairs={{8,0},{9,1},{10,2},{11,3},{12,4},{13,5},{14,6},{15,7},{16,8},{17,9... | collective-permute-start | bytes 1572872 | tf_op jit(solution)/shard_map/ppermute | solution.py:36
  211.3 126.8 %collective-permute-start.5 = (bf16[1024,256]{1,0:T(8,128)(2,1)S(1)}, bf16[1024,256]{1,0:T(8,128)(2,1)S(1)}, u32[]{:S(2)}, u32[]{:S(2)}) collective-permute-start(bf16[1024,256]{1,0:T(8,128)(2,1)S(1)} %get-tuple-element.12), channel_id=1, source_target_pairs={{24,0},{25,1},{26,2},{27,3},{28,4},{29,5},{30,6},{31,7},{32,14},{3... | collective-permute-start | bytes 1572872 | tf_op jit(solution)/shard_map/ppermute | solution.py:36
  244.5 93.5 %collective-permute-start.4 = (bf16[1024,256]{1,0:T(8,128)(2,1)S(1)}, bf16[1024,256]{1,0:T(8,128)(2,1)S(1)}, u32[]{:S(2)}, u32[]{:S(2)}) collective-permute-start(bf16[1024,256]{1,0:T(8,128)(2,1)S(1)} %get-tuple-element.13), channel_id=1, source_target_pairs={{16,0},{17,1},{18,2},{19,3},{20,4},{21,5},{22,6},{23,7},{24,8},{25... | collective-permute-start | bytes 1572872 | tf_op jit(solution)/shard_map/ppermute | solution.py:36

commit v3 on v2

--- a/solution.py
+++ b/solution.py
@@ -176,28 +176,27 @@
     tokens = queries.shape[0]
     q_cols = queries.shape[1] // uly
     kv_cols = keys.shape[1] // uly
-    packed = jnp.concatenate(
-        [
-            queries.reshape(tokens, uly, q_cols),
-            output_gradient.reshape(tokens, uly, q_cols),
-            keys.reshape(tokens, uly, kv_cols),
-            values.reshape(tokens, uly, kv_cols),
-        ],
-        axis=2,
-    )
-    packed = mirrored(packed, flip, cores)
-    packed = lax.all_to_all(packed, "uly", split_axis=1, concat_axis=0, tiled=True)
-    rows = packed.shape[0]
-    packed = packed.reshape(rows, 2 * q_cols + 2 * kv_cols)
-    queries = packed[:, :q_cols]
-    gradient = packed[:, q_cols : 2 * q_cols]
-    kv = packed[:, 2 * q_cols :]
-    groups = q_cols // HEAD_SIZE
-    softmax_scale = 1.0 / math.sqrt(HEAD_SIZE)
-
+    kv = jnp.concatenate(
+        [keys.reshape(tokens, uly, kv_cols), values.reshape(tokens, uly, kv_cols)], axis=2
+    )
+    kv = lax.all_to_all(mirrored(kv, flip, cores), "uly", split_axis=1, concat_axis=0, tiled=True)
+    rows = kv.shape[0]
+    kv = kv.reshape(rows, 2 * kv_cols)
     window = [kv]
     for step in range(1, REACH + 1):
         window.append(from_behind(kv, step, flips, cores))
+    packed = jnp.concatenate(
+        [queries.reshape(tokens, uly, q_cols), output_gradient.reshape(tokens, uly, q_cols)],
+        axis=2,
+    )
+    packed = mirrored(packed, flip, cores)
+    packed = lax.all_to_all(packed, "uly", split_axis=1, concat_axis=0, tiled=True)
+    packed = packed.reshape(rows, 2 * q_cols)
+    queries = packed[:, :q_cols]
+    gradient = packed[:, q_cols:]
+    groups = q_cols // HEAD_SIZE
+    softmax_scale = 1.0 / math.sqrt(HEAD_SIZE)
+
     window = jnp.concatenate(window[::-1], axis=0)
     key_window = window[:, :HEAD_SIZE]
     value_window = window[:, HEAD_SIZE:]
@@ -220,20 +219,31 @@
         meta, queries, gradient, key_window, value_window, q_start[:, None], groups, softmax_scale
     )
     partials = jnp.concatenate([dk_window, dv_window], axis=1)
+    returned = [
+        from_behind(
+            partials[(REACH - step) * rows : (REACH - step + 1) * rows].astype(jnp.bfloat16),
+            -step,
+            flips,
+            cores,
+        )
+        for step in range(1, REACH + 1)
+    ]
+    out_q = lax.all_to_all(dq, "uly", split_axis=0, concat_axis=1, tiled=True)
+    out_q, returned = lax.optimization_barrier((out_q, returned))
+    out_q = mirrored(out_q.reshape(out_q.shape[0], uly, q_cols), flip, cores)
     total = partials[REACH * rows :]
-    for step in range(1, REACH + 1):
-        piece = partials[(REACH - step) * rows : (REACH - step + 1) * rows]
-        total = total + from_behind(piece.astype(jnp.bfloat16), -step, flips, cores).astype(jnp.float32)
+    for piece in returned:
+        total = total + piece.astype(jnp.float32)
     out_k = (softmax_scale * total[:, :HEAD_SIZE]).astype(jnp.bfloat16)
     out_v = total[:, HEAD_SIZE:].astype(jnp.bfloat16)
-    result = jnp.concatenate([dq, out_k, out_v], axis=1)
-    result = lax.all_to_all(result, "uly", split_axis=0, concat_axis=1, tiled=True)
-    piece_cols = q_cols + 2 * kv_cols
-    result = mirrored(result.reshape(result.shape[0], uly, piece_cols), flip, cores)
+    out_kv = lax.all_to_all(
+        jnp.concatenate([out_k, out_v], axis=1), "uly", split_axis=0, concat_axis=1, tiled=True
+    )
+    out_kv = mirrored(out_kv.reshape(out_kv.shape[0], uly, 2 * kv_cols), flip, cores)
     return (
-        result[:, :, :q_cols].reshape(result.shape[0], uly * q_cols),
-        result[:, :, q_cols : q_cols + kv_cols].reshape(result.shape[0], uly * kv_cols),
-        result[:, :, q_cols + kv_cols :].reshape(result.shape[0], uly * kv_cols),
+        out_q.reshape(out_q.shape[0], uly * q_cols),
+        out_kv[:, :, :kv_cols].reshape(out_kv.shape[0], uly * kv_cols),
+        out_kv[:, :, kv_cols:].reshape(out_kv.shape[0], uly * kv_cols),
     )
 
 

time: 377 us -> 338 us (0.90)
  the two profiles are of different devices: /device:TPU:10 before, /device:TPU:22 now
where the time goes in v3:
time: 338 us; the launch traced here: 339 us
  waiting for transfers between devices  151 us (45%)
  starting transfers between devices  102 us (30%)
  Pallas kernels  48.8 us (14%)
  local copies, waits for them, and re-layouts  25.8 us (8%)
  other arithmetic  10 us (3%)
    ppermute x6, waiting for transfers between devices, from_behind(): return lax.ppermute(shard, ('ctx', 'uly'), pairs)  132 us
    ppermute x6, starting transfers between devices, from_behind(): return lax.ppermute(shard, ('ctx', 'uly'), pairs)  83.7 us
    pallas_call x1, Pallas kernels, attend(): pl.pallas_call(kernel, out_shape=(jax.ShapeDtypeStruct(queries.shape, jnp...  48.8 us
    all_to_all x1, waiting for transfers between devices, on_device(): lax.all_to_all(jnp.concatenate([out_k, out_v], axis=1), 'uly', split_axis...  13.2 us
    unnamed x17, local copies, waits for them, and re-layouts  7.18 us
  transfers between devices with their start and end apart: 10, of which 7 were waited for; matrix products, arithmetic and copies ran while one was open for 5% of the time, Pallas kernels for 0%

profile of v3, /device:TPU:22, one launch (start us, length us, event | category | flops | bytes accessed | tf_op | source)
XLA Modules:
  0.0 338.7 jit_solution(13405070331116347868)
XLA Ops:
  0.6 1.1 concatenate.32
  1.8 0.2 constant_dynamic-update-slice_fusion.3
  1.9 0.0 copy-start.4
  2.0 1.2 concatenate.33
  3.2 1.3 dynamic_slice.3
  4.4 0.4 constant_dynamic-update-slice_fusion.2
  4.8 1.2 broadcast_select_fusion.2
  6.0 0.9 copy.27
  6.9 5.9 %all-to-all-start.1 = ((bf16[128,8,256]{2,0,1:T(8,128)(2,1)}), bf16[128,8,256]{2,0,1:T(8,128)(2,1)}, u32[]{:S(2)}, u32[]{:S(2)}) async-start(bf16[128,8,256]{2,0,1:T(8,128)(2,1)} %bitcast.12), calls=%async_computation.1 | async-start | bytes 1048576 | tf_op jit(solution)/shard_map/all_to_all | solution.py:182
  12.8 0.8 concatenate.29
  13.6 1.2 constant_dynamic-update-slice_fusion.1
  14.8 1.8 concatenate.30
  16.6 0.9 constant_dynamic-update-slice_fusion
  17.5 2.8 broadcast_select_fusion
  20.3 2.5 copy.26
  22.8 5.4 %all-to-all-done.1 = bf16[128,8,256]{2,0,1:T(8,128)(2,1)} async-done(((bf16[128,8,256]{2,0,1:T(8,128)(2,1)}), bf16[128,8,256]{2,0,1:T(8,128)(2,1)}, u32[]{:S(2)}, u32[]{:S(2)}) %all-to-all-start.1) | async-done | bytes 524320 | tf_op jit(solution)/shard_map/all_to_all | solution.py:182
  28.2 4.5 %all-to-all-start = ((bf16[128,8,1024]{2,0,1:T(8,128)(2,1)}), bf16[128,8,1024]{2,0,1:T(8,128)(2,1)}, u32[]{:S(2)}, u32[]{:S(2)}) async-start(bf16[128,8,1024]{2,0,1:T(8,128)(2,1)} %bitcast.6), calls=%async_computation | async-start | bytes 4194304 | tf_op jit(solution)/shard_map/all_to_all | solution.py:193
  32.7 0.1 copy.24
  32.8 0.1 reduce-window.8
  32.9 0.1 reduce
  33.0 0.1 select_reduce_fusion
  33.1 7.6 %collective-permute-start.2 = (bf16[1024,256]{1,0:T(8,128)(2,1)}, bf16[1024,256]{1,0:T(8,128)(2,1)S(1)}, u32[]{:S(2)}, u32[]{:S(2)}) collective-permute-start(bf16[1024,256]{1,0:T(8,128)(2,1)} %bitcast.15), channel_id=1, source_target_pairs={{0,8},{1,9},{2,10},{3,11},{4,12},{5,13},{6,14},{7,15},{8,16},{9,17... | collective-permute-start | bytes 1572872 | tf_op jit(solution)/shard_map/ppermute | solution.py:36
  40.7 4.3 %collective-permute-start.1 = (bf16[1024,256]{1,0:T(8,128)(2,1)}, bf16[1024,256]{1,0:T(8,128)(2,1)S(1)}, u32[]{:S(2)}, u32[]{:S(2)}) collective-permute-start(bf16[1024,256]{1,0:T(8,128)(2,1)} %bitcast.15), channel_id=1, source_target_pairs={{0,16},{1,17},{2,18},{3,19},{4,20},{5,21},{6,22},{7,23},{8,24},{9,... | collective-permute-start | bytes 1572872 | tf_op jit(solution)/shard_map/ppermute | solution.py:36
  45.0 2.1 collective-permute-start
  47.2 0.6 gather_fusion
  47.8 0.1 copy.25
  47.9 0.1 reshape.215
  48.0 0.2 copy.28.qs_ref
  48.2 0.1 pad_add_fusion.1.meta_ref
  48.3 10.2 %collective-permute-done.2 = bf16[1024,256]{1,0:T(8,128)(2,1)S(1)} collective-permute-done((bf16[1024,256]{1,0:T(8,128)(2,1)}, bf16[1024,256]{1,0:T(8,128)(2,1)S(1)}, u32[]{:S(2)}, u32[]{:S(2)}) %collective-permute-start.2) | collective-permute-done | bytes 524320 | tf_op jit(solution)/shard_map/ppermute | solution.py:36
  58.6 22.4 %collective-permute-done.1 = bf16[1024,256]{1,0:T(8,128)(2,1)S(1)} collective-permute-done((bf16[1024,256]{1,0:T(8,128)(2,1)}, bf16[1024,256]{1,0:T(8,128)(2,1)S(1)}, u32[]{:S(2)}, u32[]{:S(2)}) %collective-permute-start.1) | collective-permute-done | bytes 524320 | tf_op jit(solution)/shard_map/ppermute | solution.py:36
  81.0 32.1 %collective-permute-done = bf16[1024,256]{1,0:T(8,128)(2,1)S(1)} collective-permute-done((bf16[1024,256]{1,0:T(8,128)(2,1)}, bf16[1024,256]{1,0:T(8,128)(2,1)S(1)}, u32[]{:S(2)}, u32[]{:S(2)}) %collective-permute-start) | collective-permute-done | bytes 524320 | tf_op jit(solution)/shard_map/ppermute | solution.py:36
  113.1 1.2 pad_maximum_fusion
  114.3 0.1 fusion.7
  114.4 0.0 all-to-all-done
  114.4 1.7 fusion.8
  116.1 48.8 %shard_map.85 = (bf16[1024,512]{1,0:T(8,128)(2,1)S(1)}, f32[4096,128]{1,0:T(8,128)}, f32[4096,128]{1,0:T(8,128)}) custom-call(s32[10]{0:T(128)S(1)} %pad_add_fusion.1.meta_ref, bf16[1024,512]{1,0:T(8,128)(2,1)S(1)} %get-tuple-element.23.q_ref, bf16[1024,512]{1,0:T(8,128)(2,1)S(1)} %get-tuple-element.22.do_ref, ...), custom_call_target="tpu_custom_call" | custom-call | tf_op jit(solution)/shard_map/pallas_call | solution.py:150
  164.9 1.0 copy-done
  165.9 2.4 copy.29
  168.3 3.6 %all-to-all-start.2 = ((bf16[8,128,512]{1,2,0:T(8,128)(2,1)}), bf16[8,128,512]{1,2,0:T(8,128)(2,1)S(1)}, u32[]{:S(2)}, u32[]{:S(2)}) async-start(bf16[8,128,512]{1,2,0:T(8,128)(2,1)} %copy.29), calls=%async_computation.2 | async-start | bytes 2097152 | tf_op jit(solution)/shard_map/all_to_all | solution.py:231
  171.9 0.2 constant_dynamic-update-slice_fusion.5
  172.0 1.4 copy-done.2
  173.5 0.2 constant_dynamic-update-slice_fusion.4
  173.6 0.2 convert.8
  173.9 1.7 copy-done.1
  175.6 0.1 fusion.6
  175.7 11.9 %collective-permute-start.5 = (bf16[1024,256]{1,0:T(8,128)(2,1)S(1)}, bf16[1024,256]{1,0:T(8,128)(2,1)S(1)}, u32[]{:S(2)}, u32[]{:S(2)}) collective-permute-start(bf16[1024,256]{1,0:T(8,128)(2,1)S(1)} %get-tuple-element.17), channel_id=1, source_target_pairs={{24,0},{25,1},{26,2},{27,3},{28,4},{29,5},{30,6},{31,7},{32,14},{3... | collective-permute-start | bytes 1572872 | tf_op jit(solution)/shard_map/ppermute | solution.py:36
  187.6 55.8 %collective-permute-start.4 = (bf16[1024,256]{1,0:T(8,128)(2,1)S(1)}, bf16[1024,256]{1,0:T(8,128)(2,1)S(1)}, u32[]{:S(2)}, u32[]{:S(2)}) collective-permute-start(bf16[1024,256]{1,0:T(8,128)(2,1)S(1)} %get-tuple-element.18), channel_id=1, source_target_pairs={{16,0},{17,1},{18,2},{19,3},{20,4},{21,5},{22,6},{23,7},{24,8},{25... | collective-permute-start | bytes 1572872 | tf_op jit(solution)/shard_map/ppermute | solution.py:36
  243.5 1.9 collective-permute-start.3
  245.4 0.0 collective-permute-done.5
  245.4 14.2 %collective-permute-done.4 = bf16[1024,256]{1,0:T(8,128)(2,1)S(1)} collective-permute-done((bf16[1024,256]{1,0:T(8,128)(2,1)S(1)}, bf16[1024,256]{1,0:T(8,128)(2,1)S(1)}, u32[]{:S(2)}, u32[]{:S(2)}) %collective-permute-start.4) | collective-permute-done | bytes 524320 | tf_op jit(solution)/shard_map/ppermute | solution.py:36
  259.7 53.0 %collective-permute-done.3 = bf16[1024,256]{1,0:T(8,128)(2,1)S(1)} collective-permute-done((bf16[1024,256]{1,0:T(8,128)(2,1)S(1)}, bf16[1024,256]{1,0:T(8,128)(2,1)S(1)}, u32[]{:S(2)}, u32[]{:S(2)}) %collective-permute-start.3) | collective-permute-done | bytes 524320 | tf_op jit(solution)/shard_map/ppermute | solution.py:36
  312.7 0.0 all-to-all-done.2
  312.7 1.4 fusion.1
  314.2 0.8 pad_maximum_fusion.1
  315.1 4.7 %all-to-all-start.3 = ((bf16[8,128,256]{2,1,0:T(8,128)(2,1)}), bf16[8,128,256]{2,1,0:T(8,128)(2,1)S(1)}, u32[]{:S(2)}, u32[]{:S(2)}) async-start(bf16[8,128,256]{2,1,0:T(8,128)(2,1)} %bitcast.24), calls=%async_computation.3 | async-start | bytes 1048576 | tf_op jit(solution)/shard_map/all_to_all | solution.py:239
  319.8 0.8 reverse_select_fusion
  320.7 1.3 copy.33
  322.0 13.2 %all-to-all-done.3 = bf16[8,128,256]{2,1,0:T(8,128)(2,1)S(1)} async-done(((bf16[8,128,256]{2,1,0:T(8,128)(2,1)}), bf16[8,128,256]{2,1,0:T(8,128)(2,1)S(1)}, u32[]{:S(2)}, u32[]{:S(2)}) %all-to-all-start.3) | async-done | bytes 524320 | tf_op jit(solution)/shard_map/all_to_all | solution.py:239
  335.2 0.5 copy.31
  335.7 1.2 broadcast_select_fusion.1
  336.9 0.2 reshape.220
  337.2 0.8 copy.38
  337.9 0.8 copy.39
  (16 shorter events, 0.2 us)
Async XLA Ops:
  1.9 10.8 %copy-start.4 = (bf16[128,4096]{1,0:T(8,128)(2,1)S(1)}, bf16[128,4096]{1,0:T(8,128)(2,1)}, u32[]{:S(2)}) copy-start(bf16[128,4096]{1,0:T(8,128)(2,1)} %param.6) | copy-start | bytes 3145732
  6.9 21.4 %all-to-all-start.1 = ((bf16[128,8,256]{2,0,1:T(8,128)(2,1)}), bf16[128,8,256]{2,0,1:T(8,128)(2,1)}, u32[]{:S(2)}, u32[]{:S(2)}) async-start(bf16[128,8,256]{2,0,1:T(8,128)(2,1)} %bitcast.12), calls=%async_computation.1 | async-start | bytes 1048576 | tf_op jit(solution)/shard_map/all_to_all | solution.py:182
  28.2 4.5 %copy-start.5 = (s32[32]{0:T(128)S(1)}, s32[32]{0:T(128)}, u32[]{:S(2)}) copy-start(s32[32]{0:T(128)} %param.10) | copy-start | bytes 388
  28.2 86.2 %all-to-all-start = ((bf16[128,8,1024]{2,0,1:T(8,128)(2,1)}), bf16[128,8,1024]{2,0,1:T(8,128)(2,1)}, u32[]{:S(2)}, u32[]{:S(2)}) async-start(bf16[128,8,1024]{2,0,1:T(8,128)(2,1)} %bitcast.6), calls=%async_computation | async-start | bytes 4194304 | tf_op jit(solution)/shard_map/all_to_all | solution.py:193
  33.1 25.5 %collective-permute-start.2 = (bf16[1024,256]{1,0:T(8,128)(2,1)}, bf16[1024,256]{1,0:T(8,128)(2,1)S(1)}, u32[]{:S(2)}, u32[]{:S(2)}) collective-permute-start(bf16[1024,256]{1,0:T(8,128)(2,1)} %bitcast.15), channel_id=1, source_target_pairs={{0,8},{1,9},{2,10},{3,11},{4,12},{5,13},{6,14},{7,15},{8,16},{9,17... | collective-permute-start | bytes 1572872 | tf_op jit(solution)/shard_map/ppermute | solution.py:36
  40.7 40.3 %collective-permute-start.1 = (bf16[1024,256]{1,0:T(8,128)(2,1)}, bf16[1024,256]{1,0:T(8,128)(2,1)S(1)}, u32[]{:S(2)}, u32[]{:S(2)}) collective-permute-start(bf16[1024,256]{1,0:T(8,128)(2,1)} %bitcast.15), channel_id=1, source_target_pairs={{0,16},{1,17},{2,18},{3,19},{4,20},{5,21},{6,22},{7,23},{8,24},{9,... | collective-permute-start | bytes 1572872 | tf_op jit(solution)/shard_map/ppermute | solution.py:36
  45.0 68.0 %collective-permute-start = (bf16[1024,256]{1,0:T(8,128)(2,1)}, bf16[1024,256]{1,0:T(8,128)(2,1)S(1)}, u32[]{:S(2)}, u32[]{:S(2)}) collective-permute-start(bf16[1024,256]{1,0:T(8,128)(2,1)} %bitcast.15), channel_id=1, source_target_pairs={{0,24},{1,25},{2,26},{3,27},{4,28},{5,29},{6,30},{7,31},{8,38},{9,... | collective-permute-start | bytes 1572872 | tf_op jit(solution)/shard_map/ppermute | solution.py:36
  164.9 1.0 copy-start
  165.9 6.0 %copy-start.3 = (f32[4096,128]{1,0:T(8,128)S(1)}, f32[4096,128]{1,0:T(8,128)}, u32[]{:S(2)}) copy-start(f32[4096,128]{1,0:T(8,128)} %get-tuple-element.11) | copy-start | bytes 6291460
  168.3 144.4 %all-to-all-start.2 = ((bf16[8,128,512]{1,2,0:T(8,128)(2,1)}), bf16[8,128,512]{1,2,0:T(8,128)(2,1)S(1)}, u32[]{:S(2)}, u32[]{:S(2)}) async-start(bf16[8,128,512]{1,2,0:T(8,128)(2,1)} %copy.29), calls=%async_computation.2 | async-start | bytes 2097152 | tf_op jit(solution)/shard_map/all_to_all | solution.py:231
  171.9 1.6 copy-start.2
  173.6 2.0 copy-start.1
  175.7 69.7 %collective-permute-start.5 = (bf16[1024,256]{1,0:T(8,128)(2,1)S(1)}, bf16[1024,256]{1,0:T(8,128)(2,1)S(1)}, u32[]{:S(2)}, u32[]{:S(2)}) collective-permute-start(bf16[1024,256]{1,0:T(8,128)(2,1)S(1)} %get-tuple-element.17), channel_id=1, source_target_pairs={{24,0},{25,1},{26,2},{27,3},{28,4},{29,5},{30,6},{31,7},{32,14},{3... | collective-permute-start | bytes 1572872 | tf_op jit(solution)/shard_map/ppermute | solution.py:36
  187.6 72.0 %collective-permute-start.4 = (bf16[1024,256]{1,0:T(8,128)(2,1)S(1)}, bf16[1024,256]{1,0:T(8,128)(2,1)S(1)}, u32[]{:S(2)}, u32[]{:S(2)}) collective-permute-start(bf16[1024,256]{1,0:T(8,128)(2,1)S(1)} %get-tuple-element.18), channel_id=1, source_target_pairs={{16,0},{17,1},{18,2},{19,3},{20,4},{21,5},{22,6},{23,7},{24,8},{25... | collective-permute-start | bytes 1572872 | tf_op jit(solution)/shard_map/ppermute | solution.py:36
  243.5 69.2 %collective-permute-start.3 = (bf16[1024,256]{1,0:T(8,128)(2,1)S(1)}, bf16[1024,256]{1,0:T(8,128)(2,1)S(1)}, u32[]{:S(2)}, u32[]{:S(2)}) collective-permute-start(bf16[1024,256]{1,0:T(8,128)(2,1)S(1)} %get-tuple-element.19), channel_id=1, source_target_pairs={{8,0},{9,1},{10,2},{11,3},{12,4},{13,5},{14,6},{15,7},{16,8},{17,9... | collective-permute-start | bytes 1572872 | tf_op jit(solution)/shard_map/ppermute | solution.py:36
  315.1 20.1 %all-to-all-start.3 = ((bf16[8,128,256]{2,1,0:T(8,128)(2,1)}), bf16[8,128,256]{2,1,0:T(8,128)(2,1)S(1)}, u32[]{:S(2)}, u32[]{:S(2)}) async-start(bf16[8,128,256]{2,1,0:T(8,128)(2,1)} %bitcast.24), calls=%async_computation.3 | async-start | bytes 1048576 | tf_op jit(solution)/shard_map/all_to_all | solution.py:239
